TPU v7x, 128 devices: a whole 4x4x4 slice. The times are simulated.
128 devices in a mesh: gx: 8 (over z, core), gy: 16 (over y, x).
Axes of the slice: x: 4, y: 4, z: 4, core: 2. Of those that a mesh axis runs over, the one named last changes fastest.
Arguments:
- initial_guess: float32 [5, 64, 512, 128], P(None, 'gx', 'gy'), may hold values from -6 to 6
- right_side: float32 [5, 64, 512, 128], P(None, 'gx', 'gy'), may hold values from -6 to 6
- coefficients: float32 [5, 64, 512, 128], P(None, 'gx', 'gy'), may hold values from 0.3 to 3
- tunnel_mask: int32 [64, 512, 128], P('gx', 'gy'), may hold values 0 or 1
- stencil: float32 [27, 5, 5], replicated, may hold values from -0.03 to 1.15, as said below
Outputs:
- fine_iterate: float32 [5, 64, 512, 128], P(None, 'gx', 'gy')
- middle_iterate: float32 [5, 32, 256, 128], P(None, 'gx', 'gy')
- lower_iterate: float32 [5, 16, 128, 128], P(None, 'gx', 'gy')
- coarse_residual: float32 [5, 8, 64, 128], P(None, 'gx', 'gy')
Inputs may be any that keep to these rules, and one draw needn't show every extreme that they name: `stencil`: entries of all 27 blocks; the centre block's diagonal lies in 0.85 to 1.15; off-centre blocks have diagonal entries in -0.025 to -0.01 and off-diagonal entries in -0.004 to 0.004; the centre block's off-diagonal entries lie in -0.02 to 0.02.
All inputs are finite; a program needn't handle non-finite values. No bound on the sum of `tunnel_mask` on one device may be relied on, other than what follows from the above.
Results may differ from a plain program's by a relative error of at most 0.00029.
Values sent between devices are 32-bit elements; how exact they have to be, the bound alone decides.
No kernel may reach another device: no remote copies, remote signals or barrier semaphores. Data moves between devices by JAX's collectives and lax.ppermute only.
A program may use at most 64 MiB of HBM per device.

v0:
```python
import jax
import jax.numpy as jnp
from jax import lax
from jax.sharding import PartitionSpec as P

SWEEPS = 2


DAMPING = 0.7
WEIGHTS = (0.125, 0.375, 0.375, 0.125)


def with_halo(block, sides, width):
    for axis, dim in sides:
        count = lax.axis_size(axis)
        forward = [(i, i + 1) for i in range(count - 1)]
        backward = [(target, source) for source, target in forward]
        low = lax.ppermute(
            lax.slice_in_dim(block, block.shape[dim] - width, None, axis=dim), axis, forward
        )
        high = lax.ppermute(lax.slice_in_dim(block, 0, width, axis=dim), axis, backward)
        block = jnp.concatenate([low, block, high], axis=dim)
    return block


def face_fine(values):
    return with_halo(values, (("gx", 1), ("gy", 2)), 1)


def face_coarse(values):
    return with_halo(values, (("gx", 1), ("gy", 2)), 1)


def face_thin(values):
    return with_halo(values, (("gx", 1), ("gy", 2)), 1)


def face_residual(values):
    return with_halo(values, (("gx", 1), ("gy", 2)), 1)


def operate(iterate, conduct, rock_share, stencil, faces):
    masked = rock_share[None] * iterate
    padded = jnp.pad(faces(masked), ((0, 0), (0, 0), (0, 0), (1, 1)))
    extent_x, extent_y, extent_z = (iterate.shape[1], iterate.shape[2], iterate.shape[3])
    summed = jnp.zeros(iterate.shape, jnp.float32)
    for offset in range(27):
        shift_x, shift_y, shift_z = (offset // 9, offset // 3 % 3, offset % 3)
        shifted = padded[
            :,
            shift_x : shift_x + extent_x,
            shift_y : shift_y + extent_y,
            shift_z : shift_z + extent_z,
        ]
        summed = summed + jnp.einsum(
            "ab,bxyz->axyz", stencil[offset], shifted, precision=lax.Precision.HIGHEST
        )
    return conduct * rock_share[None] * summed


def smooth_level(iterate, forcing, conduct, rock_share, stencil, faces):
    diagonal = conduct * jnp.diagonal(stencil[13])[:, None, None, None]
    source = rock_share[None] * forcing
    if iterate is None:
        iterate = DAMPING * source / diagonal
        remaining = SWEEPS - 1
    else:
        remaining = SWEEPS
    for sweep_index in range(remaining):
        iterate = (
            iterate
            + DAMPING * (source - operate(iterate, conduct, rock_share, stencil, faces)) / diagonal
        )
    residual = source - operate(iterate, conduct, rock_share, stencil, faces)
    return (iterate, residual)


def shrink(padded):
    extent_x = padded.shape[1] - 2
    along_x = sum(
        (
            WEIGHTS[weight_index] * padded[:, weight_index : weight_index + extent_x - 1 : 2]
            for weight_index in range(4)
        )
    )
    extent_y = padded.shape[2] - 2
    return sum(
        (
            WEIGHTS[weight_index] * along_x[:, :, weight_index : weight_index + extent_y - 1 : 2]
            for weight_index in range(4)
        )
    )


def restrict(values):
    return shrink(face_residual(values))


def coarsen(values):
    leading = values.shape[:-3]
    extent_x, extent_y, extent_z = (values.shape[-3], values.shape[-2], values.shape[-1])
    reshaped = values.reshape(leading + (extent_x // 2, 2, extent_y // 2, 2, extent_z))
    return reshaped.mean(axis=(-4, -2))


def body(initial_guess, right_side, coefficients, tunnel_mask, stencil):
    rock_share = tunnel_mask.astype(jnp.float32)
    conduct = coefficients
    fine_iterate, residual = smooth_level(
        initial_guess, right_side, conduct, rock_share, stencil, face_fine
    )
    kept = [fine_iterate]
    for layer_index in range(2):
        forcing = restrict(residual)
        conduct = coarsen(conduct)
        rock_share = coarsen(rock_share)
        iterate, residual = smooth_level(None, forcing, conduct, rock_share, stencil, face_coarse)
        kept.append(iterate)
    forcing = restrict(residual)
    conduct = coarsen(conduct)
    rock_share = coarsen(rock_share)
    iterate, coarse_residual = smooth_level(None, forcing, conduct, rock_share, stencil, face_thin)
    return (kept[0], kept[1], kept[2], coarse_residual)


def solution(mesh):
    placed = (
        P(None, "gx", "gy", None),
        P(None, "gx", "gy", None),
        P(None, "gx", "gy", None),
        P("gx", "gy", None),
        P(),
    )
    return jax.shard_map(
        body,
        mesh=mesh,
        in_specs=placed,
        out_specs=(
            P(None, "gx", "gy", None),
            P(None, "gx", "gy", None),
            P(None, "gx", "gy", None),
            P(None, "gx", "gy", None),
        ),
        check_vma=False,
    )
```

profile of v0, /device:TPU:41, one launch (start us, length us, event | category | flops | bytes accessed | tf_op | source)
XLA Modules:
  0.0 354.8 jit_solution(14806816911237174016)
XLA Ops:
  3.1 4.2 %collective-permute-start = (f32[5,1,32,128]{3,0,2,1:T(8,128)S(1)}, f32[5,1,32,128]{3,0,2,1:T(8,128)S(1)}, u32[]{:S(2)}, u32[]{:S(2)}) collective-permute-start(f32[5,1,32,128]{3,0,2,1:T(8,128)S(1)} %get-tuple-element.48), channel_id=1, source_target_pairs={{0,16},{16,32},{32,48},{48,64},{64,80},{80,96},{96,112},{1,17},{17... | collective-permute-start | bytes 245768 | tf_op jit(solution)/shard_map/ppermute | solution.py:18
  16.4 3.1 collective-permute-start.2
  19.5 4.7 %collective-permute-start.3 = (f32[5,10,1,128]{3,0,2,1:T(8,128)S(1)}, f32[5,10,1,128]{3,0,2,1:T(8,128)S(1)}, u32[]{:S(2)}, u32[]{:S(2)}) collective-permute-start(f32[5,10,1,128]{3,0,2,1:T(8,128)S(1)} %get-tuple-element.41), channel_id=1, source_target_pairs={{1,0},{2,1},{3,2},{4,3},{5,4},{6,5},{7,6},{8,7},{9,8},{10,9},{11,1... | collective-permute-start | bytes 76808 | tf_op jit(solution)/shard_map/ppermute | solution.py:21
  56.7 4.2 %collective-permute-start.4 = (f32[5,1,32,128]{3,0,2,1:T(8,128)S(1)}, f32[5,1,32,128]{3,0,2,1:T(8,128)S(1)}, u32[]{:S(2)}, u32[]{:S(2)}) collective-permute-start(f32[5,1,32,128]{3,0,2,1:T(8,128)S(1)} %get-tuple-element.46), channel_id=1, source_target_pairs={{0,16},{16,32},{32,48},{48,64},{64,80},{80,96},{96,112},{1,17},{17... | collective-permute-start | bytes 245768 | tf_op jit(solution)/shard_map/ppermute | solution.py:18
  63.8 3.3 collective-permute-done.5
  69.1 5.9 %collective-permute-start.7 = (f32[5,10,1,128]{3,0,2,1:T(8,128)S(1)}, f32[5,10,1,128]{3,0,2,1:T(8,128)S(1)}, u32[]{:S(2)}, u32[]{:S(2)}) collective-permute-start(f32[5,10,1,128]{3,0,2,1:T(8,128)S(1)} %get-tuple-element.39), channel_id=1, source_target_pairs={{1,0},{2,1},{3,2},{4,3},{5,4},{6,5},{7,6},{8,7},{9,8},{10,9},{11,1... | collective-permute-start | bytes 76808 | tf_op jit(solution)/shard_map/ppermute | solution.py:21
  103.9 3.8 %broadcast_multiply_fusion = (f32[5,8,32,128]{3,0,2,1:T(8,128)S(1)}, f32[5,8,32,128]{3,0,2,1:T(8,128)}) fusion(f32[8,32,128]{2,1,0:T(8,128)S(1)} %convert_element_type.16, f32[5,8,32,128]{3,0,2,1:T(8,128)S(1)} %get-tuple-element.113, f32[5]{0:T(128)S(1)} %gather_fusion, f32[5,8,32,128]{3,0,2,1:T(8,128)S(1)} %convolution_bitcast_fusion.16, ...), kind=kOutput, calls=%fused_computation.510 | convolution fusion | flops 13434880 | bytes 18485760 | tf_op jit(solution)/shard_map/ab,bxyz->axyz/dot_general | solution.py:55
  113.1 3.3 collective-permute-done.9
  118.3 5.8 %collective-permute-start.11 = (f32[5,10,1,128]{3,0,2,1:T(8,128)S(1)}, f32[5,10,1,128]{3,0,2,1:T(8,128)S(1)}, u32[]{:S(2)}, u32[]{:S(2)}) collective-permute-start(f32[5,10,1,128]{3,0,2,1:T(8,128)S(1)} %get-tuple-element.37), channel_id=1, source_target_pairs={{1,0},{2,1},{3,2},{4,3},{5,4},{6,5},{7,6},{8,7},{9,8},{10,9},{11,1... | collective-permute-start | bytes 76808 | tf_op jit(solution)/shard_map/ppermute | solution.py:21
  160.3 4.3 %collective-permute-done.13 = f32[5,1,32,128]{3,0,2,1:T(8,128)S(1)} collective-permute-done((f32[5,1,32,128]{3,0,2,1:T(8,128)S(1)}, f32[5,1,32,128]{3,0,2,1:T(8,128)S(1)}, u32[]{:S(2)}, u32[]{:S(2)}) %collective-permute-start.13) | collective-permute-done | bytes 81952 | tf_op jit(solution)/shard_map/ppermute | solution.py:21
  166.6 5.4 %collective-permute-start.15 = (f32[5,10,1,128]{3,0,2,1:T(8,128)S(1)}, f32[5,10,1,128]{3,0,2,1:T(8,128)S(1)}, u32[]{:S(2)}, u32[]{:S(2)}) collective-permute-start(f32[5,10,1,128]{3,0,2,1:T(8,128)S(1)} %get-tuple-element.35), channel_id=1, source_target_pairs={{1,0},{2,1},{3,2},{4,3},{5,4},{6,5},{7,6},{8,7},{9,8},{10,9},{11,1... | collective-permute-start | bytes 76808 | tf_op jit(solution)/shard_map/ppermute | solution.py:21
  178.4 3.6 %collective-permute-done.17 = f32[5,1,16,128]{3,0,2,1:T(8,128)S(1)} collective-permute-done((f32[5,1,16,128]{3,0,2,1:T(8,128)S(1)}, f32[5,1,16,128]{3,0,2,1:T(8,128)S(1)}, u32[]{:S(2)}, u32[]{:S(2)}) %collective-permute-start.17) | collective-permute-done | bytes 40992 | tf_op jit(solution)/shard_map/ppermute | solution.py:21
  184.9 5.5 %collective-permute-start.19 = (f32[5,6,1,128]{3,0,2,1:T(8,128)S(1)}, f32[5,6,1,128]{3,0,2,1:T(8,128)S(1)}, u32[]{:S(2)}, u32[]{:S(2)}) collective-permute-start(f32[5,6,1,128]{3,0,2,1:T(8,128)S(1)} %get-tuple-element.55), channel_id=1, source_target_pairs={{1,0},{2,1},{3,2},{4,3},{5,4},{6,5},{7,6},{8,7},{9,8},{10,9},{11,1... | collective-permute-start | bytes 46088 | tf_op jit(solution)/shard_map/ppermute | solution.py:21
  206.4 3.6 %collective-permute-done.21 = f32[5,1,16,128]{3,0,2,1:T(8,128)S(1)} collective-permute-done((f32[5,1,16,128]{3,0,2,1:T(8,128)S(1)}, f32[5,1,16,128]{3,0,2,1:T(8,128)S(1)}, u32[]{:S(2)}, u32[]{:S(2)}) %collective-permute-start.21) | collective-permute-done | bytes 40992 | tf_op jit(solution)/shard_map/ppermute | solution.py:21
  210.0 3.4 collective-permute-start.22
  213.5 4.7 %collective-permute-start.23 = (f32[5,6,1,128]{3,0,2,1:T(8,128)S(1)}, f32[5,6,1,128]{3,0,2,1:T(8,128)S(1)}, u32[]{:S(2)}, u32[]{:S(2)}) collective-permute-start(f32[5,6,1,128]{3,0,2,1:T(8,128)S(1)} %get-tuple-element.53), channel_id=1, source_target_pairs={{1,0},{2,1},{3,2},{4,3},{5,4},{6,5},{7,6},{8,7},{9,8},{10,9},{11,1... | collective-permute-start | bytes 46088 | tf_op jit(solution)/shard_map/ppermute | solution.py:21
  234.3 3.6 %collective-permute-done.25 = f32[5,1,16,128]{3,0,2,1:T(8,128)S(1)} collective-permute-done((f32[5,1,16,128]{3,0,2,1:T(8,128)S(1)}, f32[5,1,16,128]{3,0,2,1:T(8,128)S(1)}, u32[]{:S(2)}, u32[]{:S(2)}) %collective-permute-start.25) | collective-permute-done | bytes 40992 | tf_op jit(solution)/shard_map/ppermute | solution.py:21
  237.9 3.4 collective-permute-start.26
  241.3 4.5 %collective-permute-start.27 = (f32[5,6,1,128]{3,0,2,1:T(8,128)S(1)}, f32[5,6,1,128]{3,0,2,1:T(8,128)S(1)}, u32[]{:S(2)}, u32[]{:S(2)}) collective-permute-start(f32[5,6,1,128]{3,0,2,1:T(8,128)S(1)} %get-tuple-element.51), channel_id=1, source_target_pairs={{1,0},{2,1},{3,2},{4,3},{5,4},{6,5},{7,6},{8,7},{9,8},{10,9},{11,1... | collective-permute-start | bytes 46088 | tf_op jit(solution)/shard_map/ppermute | solution.py:21
  251.6 3.3 collective-permute-done.29
  254.9 3.4 collective-permute-start.30
  258.4 4.7 %collective-permute-start.31 = (f32[5,4,1,128]{3,0,2,1:T(8,128)S(1)}, f32[5,4,1,128]{3,0,2,1:T(8,128)S(1)}, u32[]{:S(2)}, u32[]{:S(2)}) collective-permute-start(f32[5,4,1,128]{3,0,2,1:T(8,128)S(1)} %get-tuple-element.67), channel_id=1, source_target_pairs={{1,0},{2,1},{3,2},{4,3},{5,4},{6,5},{7,6},{8,7},{9,8},{10,9},{11,1... | collective-permute-start | bytes 30728 | tf_op jit(solution)/shard_map/ppermute | solution.py:21
  274.5 3.3 collective-permute-done.33
  277.8 3.4 collective-permute-start.34
  281.2 4.5 %collective-permute-start.35 = (f32[5,4,1,128]{3,0,2,1:T(8,128)S(1)}, f32[5,4,1,128]{3,0,2,1:T(8,128)S(1)}, u32[]{:S(2)}, u32[]{:S(2)}) collective-permute-start(f32[5,4,1,128]{3,0,2,1:T(8,128)S(1)} %get-tuple-element.65), channel_id=1, source_target_pairs={{1,0},{2,1},{3,2},{4,3},{5,4},{6,5},{7,6},{8,7},{9,8},{10,9},{11,1... | collective-permute-start | bytes 30728 | tf_op jit(solution)/shard_map/ppermute | solution.py:21
  297.3 3.3 collective-permute-done.37
  300.6 3.4 collective-permute-start.38
  304.1 4.5 %collective-permute-start.39 = (f32[5,4,1,128]{3,0,2,1:T(8,128)S(1)}, f32[5,4,1,128]{3,0,2,1:T(8,128)S(1)}, u32[]{:S(2)}, u32[]{:S(2)}) collective-permute-start(f32[5,4,1,128]{3,0,2,1:T(8,128)S(1)} %get-tuple-element.63), channel_id=1, source_target_pairs={{1,0},{2,1},{3,2},{4,3},{5,4},{6,5},{7,6},{8,7},{9,8},{10,9},{11,1... | collective-permute-start | bytes 30728 | tf_op jit(solution)/shard_map/ppermute | solution.py:21
  317.4 3.4 collective-permute-start.42
  320.8 4.5 %collective-permute-start.43 = (f32[5,3,1,128]{3,0,2,1:T(8,128)S(1)}, f32[5,3,1,128]{3,0,2,1:T(8,128)S(1)}, u32[]{:S(2)}, u32[]{:S(2)}) collective-permute-start(f32[5,3,1,128]{3,0,2,1:T(8,128)S(1)} %get-tuple-element.77), channel_id=1, source_target_pairs={{1,0},{2,1},{3,2},{4,3},{5,4},{6,5},{7,6},{8,7},{9,8},{10,9},{11,1... | collective-permute-start | bytes 23048 | tf_op jit(solution)/shard_map/ppermute | solution.py:21
  338.9 3.4 collective-permute-start.46
  342.3 4.5 %collective-permute-start.47 = (f32[5,3,1,128]{3,0,2,1:T(8,128)S(1)}, f32[5,3,1,128]{3,0,2,1:T(8,128)S(1)}, u32[]{:S(2)}, u32[]{:S(2)}) collective-permute-start(f32[5,3,1,128]{3,0,2,1:T(8,128)S(1)} %get-tuple-element.75), channel_id=1, source_target_pairs={{1,0},{2,1},{3,2},{4,3},{5,4},{6,5},{7,6},{8,7},{9,8},{10,9},{11,1... | collective-permute-start | bytes 23048 | tf_op jit(solution)/shard_map/ppermute | solution.py:21
  (408 shorter events, 221.3 us)
Async XLA Ops:
  3.1 13.2 %collective-permute-start = (f32[5,1,32,128]{3,0,2,1:T(8,128)S(1)}, f32[5,1,32,128]{3,0,2,1:T(8,128)S(1)}, u32[]{:S(2)}, u32[]{:S(2)}) collective-permute-start(f32[5,1,32,128]{3,0,2,1:T(8,128)S(1)} %get-tuple-element.48), channel_id=1, source_target_pairs={{0,16},{16,32},{32,48},{48,64},{64,80},{80,96},{96,112},{1,17},{17... | collective-permute-start | bytes 245768 | tf_op jit(solution)/shard_map/ppermute | solution.py:18
  7.4 9.0 %collective-permute-start.1 = (f32[5,1,32,128]{3,0,2,1:T(8,128)S(1)}, f32[5,1,32,128]{3,0,2,1:T(8,128)S(1)}, u32[]{:S(2)}, u32[]{:S(2)}) collective-permute-start(f32[5,1,32,128]{3,0,2,1:T(8,128)S(1)} %get-tuple-element.49), channel_id=1, source_target_pairs={{16,0},{32,16},{48,32},{64,48},{80,64},{96,80},{112,96},{17,1},{33... | collective-permute-start | bytes 245768 | tf_op jit(solution)/shard_map/ppermute | solution.py:21
  16.4 10.0 %collective-permute-start.2 = (f32[5,10,1,128]{3,0,2,1:T(8,128)S(1)}, f32[5,10,1,128]{3,0,2,1:T(8,128)S(1)}, u32[]{:S(2)}, u32[]{:S(2)}) collective-permute-start(f32[5,10,1,128]{3,0,2,1:T(8,128)S(1)} %get-tuple-element.40), channel_id=1, source_target_pairs={{0,1},{1,2},{2,3},{3,4},{4,5},{5,6},{6,7},{7,8},{8,9},{9,10},{10,1... | collective-permute-start | bytes 76808 | tf_op jit(solution)/shard_map/ppermute | solution.py:18
  19.5 6.9 %collective-permute-start.3 = (f32[5,10,1,128]{3,0,2,1:T(8,128)S(1)}, f32[5,10,1,128]{3,0,2,1:T(8,128)S(1)}, u32[]{:S(2)}, u32[]{:S(2)}) collective-permute-start(f32[5,10,1,128]{3,0,2,1:T(8,128)S(1)} %get-tuple-element.41), channel_id=1, source_target_pairs={{1,0},{2,1},{3,2},{4,3},{5,4},{6,5},{7,6},{8,7},{9,8},{10,9},{11,1... | collective-permute-start | bytes 76808 | tf_op jit(solution)/shard_map/ppermute | solution.py:21
  56.7 7.2 %collective-permute-start.4 = (f32[5,1,32,128]{3,0,2,1:T(8,128)S(1)}, f32[5,1,32,128]{3,0,2,1:T(8,128)S(1)}, u32[]{:S(2)}, u32[]{:S(2)}) collective-permute-start(f32[5,1,32,128]{3,0,2,1:T(8,128)S(1)} %get-tuple-element.46), channel_id=1, source_target_pairs={{0,16},{16,32},{32,48},{48,64},{64,80},{80,96},{96,112},{1,17},{17... | collective-permute-start | bytes 245768 | tf_op jit(solution)/shard_map/ppermute | solution.py:18
  60.9 6.3 %collective-permute-start.5 = (f32[5,1,32,128]{3,0,2,1:T(8,128)S(1)}, f32[5,1,32,128]{3,0,2,1:T(8,128)S(1)}, u32[]{:S(2)}, u32[]{:S(2)}) collective-permute-start(f32[5,1,32,128]{3,0,2,1:T(8,128)S(1)} %get-tuple-element.47), channel_id=1, source_target_pairs={{16,0},{32,16},{48,32},{64,48},{80,64},{96,80},{112,96},{17,1},{33... | collective-permute-start | bytes 245768 | tf_op jit(solution)/shard_map/ppermute | solution.py:21
  67.2 9.9 %collective-permute-start.6 = (f32[5,10,1,128]{3,0,2,1:T(8,128)S(1)}, f32[5,10,1,128]{3,0,2,1:T(8,128)S(1)}, u32[]{:S(2)}, u32[]{:S(2)}) collective-permute-start(f32[5,10,1,128]{3,0,2,1:T(8,128)S(1)} %get-tuple-element.38), channel_id=1, source_target_pairs={{0,1},{1,2},{2,3},{3,4},{4,5},{5,6},{6,7},{7,8},{8,9},{9,10},{10,1... | collective-permute-start | bytes 76808 | tf_op jit(solution)/shard_map/ppermute | solution.py:18
  69.1 8.0 %collective-permute-start.7 = (f32[5,10,1,128]{3,0,2,1:T(8,128)S(1)}, f32[5,10,1,128]{3,0,2,1:T(8,128)S(1)}, u32[]{:S(2)}, u32[]{:S(2)}) collective-permute-start(f32[5,10,1,128]{3,0,2,1:T(8,128)S(1)} %get-tuple-element.39), channel_id=1, source_target_pairs={{1,0},{2,1},{3,2},{4,3},{5,4},{6,5},{7,6},{8,7},{9,8},{10,9},{11,1... | collective-permute-start | bytes 76808 | tf_op jit(solution)/shard_map/ppermute | solution.py:21
  110.0 6.3 %collective-permute-start.9 = (f32[5,1,32,128]{3,0,2,1:T(8,128)S(1)}, f32[5,1,32,128]{3,0,2,1:T(8,128)S(1)}, u32[]{:S(2)}, u32[]{:S(2)}) collective-permute-start(f32[5,1,32,128]{3,0,2,1:T(8,128)S(1)} %get-tuple-element.45), channel_id=1, source_target_pairs={{16,0},{32,16},{48,32},{64,48},{80,64},{96,80},{112,96},{17,1},{33... | collective-permute-start | bytes 245768 | tf_op jit(solution)/shard_map/ppermute | solution.py:21
  116.3 9.9 %collective-permute-start.10 = (f32[5,10,1,128]{3,0,2,1:T(8,128)S(1)}, f32[5,10,1,128]{3,0,2,1:T(8,128)S(1)}, u32[]{:S(2)}, u32[]{:S(2)}) collective-permute-start(f32[5,10,1,128]{3,0,2,1:T(8,128)S(1)} %get-tuple-element.36), channel_id=1, source_target_pairs={{0,1},{1,2},{2,3},{3,4},{4,5},{5,6},{6,7},{7,8},{8,9},{9,10},{10,1... | collective-permute-start | bytes 76808 | tf_op jit(solution)/shard_map/ppermute | solution.py:18
  118.3 8.0 %collective-permute-start.11 = (f32[5,10,1,128]{3,0,2,1:T(8,128)S(1)}, f32[5,10,1,128]{3,0,2,1:T(8,128)S(1)}, u32[]{:S(2)}, u32[]{:S(2)}) collective-permute-start(f32[5,10,1,128]{3,0,2,1:T(8,128)S(1)} %get-tuple-element.37), channel_id=1, source_target_pairs={{1,0},{2,1},{3,2},{4,3},{5,4},{6,5},{7,6},{8,7},{9,8},{10,9},{11,1... | collective-permute-start | bytes 76808 | tf_op jit(solution)/shard_map/ppermute | solution.py:21
  158.2 6.3 %collective-permute-start.13 = (f32[5,1,32,128]{3,0,2,1:T(8,128)S(1)}, f32[5,1,32,128]{3,0,2,1:T(8,128)S(1)}, u32[]{:S(2)}, u32[]{:S(2)}) collective-permute-start(f32[5,1,32,128]{3,0,2,1:T(8,128)S(1)} %get-tuple-element.43), channel_id=1, source_target_pairs={{16,0},{32,16},{48,32},{64,48},{80,64},{96,80},{112,96},{17,1},{33... | collective-permute-start | bytes 245768 | tf_op jit(solution)/shard_map/ppermute | solution.py:21
  164.5 7.9 %collective-permute-start.14 = (f32[5,10,1,128]{3,0,2,1:T(8,128)S(1)}, f32[5,10,1,128]{3,0,2,1:T(8,128)S(1)}, u32[]{:S(2)}, u32[]{:S(2)}) collective-permute-start(f32[5,10,1,128]{3,0,2,1:T(8,128)S(1)} %get-tuple-element.34), channel_id=1, source_target_pairs={{0,1},{1,2},{2,3},{3,4},{4,5},{5,6},{6,7},{7,8},{8,9},{9,10},{10,1... | collective-permute-start | bytes 76808 | tf_op jit(solution)/shard_map/ppermute | solution.py:18
  166.6 6.5 %collective-permute-start.15 = (f32[5,10,1,128]{3,0,2,1:T(8,128)S(1)}, f32[5,10,1,128]{3,0,2,1:T(8,128)S(1)}, u32[]{:S(2)}, u32[]{:S(2)}) collective-permute-start(f32[5,10,1,128]{3,0,2,1:T(8,128)S(1)} %get-tuple-element.35), channel_id=1, source_target_pairs={{1,0},{2,1},{3,2},{4,3},{5,4},{6,5},{7,6},{8,7},{9,8},{10,9},{11,1... | collective-permute-start | bytes 76808 | tf_op jit(solution)/shard_map/ppermute | solution.py:21
  176.4 5.6 %collective-permute-start.17 = (f32[5,1,16,128]{3,0,2,1:T(8,128)S(1)}, f32[5,1,16,128]{3,0,2,1:T(8,128)S(1)}, u32[]{:S(2)}, u32[]{:S(2)}) collective-permute-start(f32[5,1,16,128]{3,0,2,1:T(8,128)S(1)} %get-tuple-element.61), channel_id=1, source_target_pairs={{16,0},{32,16},{48,32},{64,48},{80,64},{96,80},{112,96},{17,1},{33... | collective-permute-start | bytes 122888 | tf_op jit(solution)/shard_map/ppermute | solution.py:21
  182.0 8.8 %collective-permute-start.18 = (f32[5,6,1,128]{3,0,2,1:T(8,128)S(1)}, f32[5,6,1,128]{3,0,2,1:T(8,128)S(1)}, u32[]{:S(2)}, u32[]{:S(2)}) collective-permute-start(f32[5,6,1,128]{3,0,2,1:T(8,128)S(1)} %get-tuple-element.54), channel_id=1, source_target_pairs={{0,1},{1,2},{2,3},{3,4},{4,5},{5,6},{6,7},{7,8},{8,9},{9,10},{10,1... | collective-permute-start | bytes 46088 | tf_op jit(solution)/shard_map/ppermute | solution.py:18
  184.9 6.0 %collective-permute-start.19 = (f32[5,6,1,128]{3,0,2,1:T(8,128)S(1)}, f32[5,6,1,128]{3,0,2,1:T(8,128)S(1)}, u32[]{:S(2)}, u32[]{:S(2)}) collective-permute-start(f32[5,6,1,128]{3,0,2,1:T(8,128)S(1)} %get-tuple-element.55), channel_id=1, source_target_pairs={{1,0},{2,1},{3,2},{4,3},{5,4},{6,5},{7,6},{8,7},{9,8},{10,9},{11,1... | collective-permute-start | bytes 46088 | tf_op jit(solution)/shard_map/ppermute | solution.py:21
  204.4 5.6 %collective-permute-start.21 = (f32[5,1,16,128]{3,0,2,1:T(8,128)S(1)}, f32[5,1,16,128]{3,0,2,1:T(8,128)S(1)}, u32[]{:S(2)}, u32[]{:S(2)}) collective-permute-start(f32[5,1,16,128]{3,0,2,1:T(8,128)S(1)} %get-tuple-element.59), channel_id=1, source_target_pairs={{16,0},{32,16},{48,32},{64,48},{80,64},{96,80},{112,96},{17,1},{33... | collective-permute-start | bytes 122888 | tf_op jit(solution)/shard_map/ppermute | solution.py:21
  210.0 8.5 %collective-permute-start.22 = (f32[5,6,1,128]{3,0,2,1:T(8,128)S(1)}, f32[5,6,1,128]{3,0,2,1:T(8,128)S(1)}, u32[]{:S(2)}, u32[]{:S(2)}) collective-permute-start(f32[5,6,1,128]{3,0,2,1:T(8,128)S(1)} %get-tuple-element.52), channel_id=1, source_target_pairs={{0,1},{1,2},{2,3},{3,4},{4,5},{5,6},{6,7},{7,8},{8,9},{9,10},{10,1... | collective-permute-start | bytes 46088 | tf_op jit(solution)/shard_map/ppermute | solution.py:18
  213.5 5.5 %collective-permute-start.23 = (f32[5,6,1,128]{3,0,2,1:T(8,128)S(1)}, f32[5,6,1,128]{3,0,2,1:T(8,128)S(1)}, u32[]{:S(2)}, u32[]{:S(2)}) collective-permute-start(f32[5,6,1,128]{3,0,2,1:T(8,128)S(1)} %get-tuple-element.53), channel_id=1, source_target_pairs={{1,0},{2,1},{3,2},{4,3},{5,4},{6,5},{7,6},{8,7},{9,8},{10,9},{11,1... | collective-permute-start | bytes 46088 | tf_op jit(solution)/shard_map/ppermute | solution.py:21
  232.3 5.6 %collective-permute-start.25 = (f32[5,1,16,128]{3,0,2,1:T(8,128)S(1)}, f32[5,1,16,128]{3,0,2,1:T(8,128)S(1)}, u32[]{:S(2)}, u32[]{:S(2)}) collective-permute-start(f32[5,1,16,128]{3,0,2,1:T(8,128)S(1)} %get-tuple-element.57), channel_id=1, source_target_pairs={{16,0},{32,16},{48,32},{64,48},{80,64},{96,80},{112,96},{17,1},{33... | collective-permute-start | bytes 122888 | tf_op jit(solution)/shard_map/ppermute | solution.py:21
  237.9 8.1 %collective-permute-start.26 = (f32[5,6,1,128]{3,0,2,1:T(8,128)S(1)}, f32[5,6,1,128]{3,0,2,1:T(8,128)S(1)}, u32[]{:S(2)}, u32[]{:S(2)}) collective-permute-start(f32[5,6,1,128]{3,0,2,1:T(8,128)S(1)} %get-tuple-element.50), channel_id=1, source_target_pairs={{0,1},{1,2},{2,3},{3,4},{4,5},{5,6},{6,7},{7,8},{8,9},{9,10},{10,1... | collective-permute-start | bytes 46088 | tf_op jit(solution)/shard_map/ppermute | solution.py:18
  241.3 5.5 %collective-permute-start.27 = (f32[5,6,1,128]{3,0,2,1:T(8,128)S(1)}, f32[5,6,1,128]{3,0,2,1:T(8,128)S(1)}, u32[]{:S(2)}, u32[]{:S(2)}) collective-permute-start(f32[5,6,1,128]{3,0,2,1:T(8,128)S(1)} %get-tuple-element.51), channel_id=1, source_target_pairs={{1,0},{2,1},{3,2},{4,3},{5,4},{6,5},{7,6},{8,7},{9,8},{10,9},{11,1... | collective-permute-start | bytes 46088 | tf_op jit(solution)/shard_map/ppermute | solution.py:21
  254.9 8.4 %collective-permute-start.30 = (f32[5,4,1,128]{3,0,2,1:T(8,128)S(1)}, f32[5,4,1,128]{3,0,2,1:T(8,128)S(1)}, u32[]{:S(2)}, u32[]{:S(2)}) collective-permute-start(f32[5,4,1,128]{3,0,2,1:T(8,128)S(1)} %get-tuple-element.66), channel_id=1, source_target_pairs={{0,1},{1,2},{2,3},{3,4},{4,5},{5,6},{6,7},{7,8},{8,9},{9,10},{10,1... | collective-permute-start | bytes 30728 | tf_op jit(solution)/shard_map/ppermute | solution.py:18
  258.4 5.4 %collective-permute-start.31 = (f32[5,4,1,128]{3,0,2,1:T(8,128)S(1)}, f32[5,4,1,128]{3,0,2,1:T(8,128)S(1)}, u32[]{:S(2)}, u32[]{:S(2)}) collective-permute-start(f32[5,4,1,128]{3,0,2,1:T(8,128)S(1)} %get-tuple-element.67), channel_id=1, source_target_pairs={{1,0},{2,1},{3,2},{4,3},{5,4},{6,5},{7,6},{8,7},{9,8},{10,9},{11,1... | collective-permute-start | bytes 30728 | tf_op jit(solution)/shard_map/ppermute | solution.py:21
  277.8 8.2 %collective-permute-start.34 = (f32[5,4,1,128]{3,0,2,1:T(8,128)S(1)}, f32[5,4,1,128]{3,0,2,1:T(8,128)S(1)}, u32[]{:S(2)}, u32[]{:S(2)}) collective-permute-start(f32[5,4,1,128]{3,0,2,1:T(8,128)S(1)} %get-tuple-element.64), channel_id=1, source_target_pairs={{0,1},{1,2},{2,3},{3,4},{4,5},{5,6},{6,7},{7,8},{8,9},{9,10},{10,1... | collective-permute-start | bytes 30728 | tf_op jit(solution)/shard_map/ppermute | solution.py:18
  281.2 5.4 %collective-permute-start.35 = (f32[5,4,1,128]{3,0,2,1:T(8,128)S(1)}, f32[5,4,1,128]{3,0,2,1:T(8,128)S(1)}, u32[]{:S(2)}, u32[]{:S(2)}) collective-permute-start(f32[5,4,1,128]{3,0,2,1:T(8,128)S(1)} %get-tuple-element.65), channel_id=1, source_target_pairs={{1,0},{2,1},{3,2},{4,3},{5,4},{6,5},{7,6},{8,7},{9,8},{10,9},{11,1... | collective-permute-start | bytes 30728 | tf_op jit(solution)/shard_map/ppermute | solution.py:21
  300.6 8.0 %collective-permute-start.38 = (f32[5,4,1,128]{3,0,2,1:T(8,128)S(1)}, f32[5,4,1,128]{3,0,2,1:T(8,128)S(1)}, u32[]{:S(2)}, u32[]{:S(2)}) collective-permute-start(f32[5,4,1,128]{3,0,2,1:T(8,128)S(1)} %get-tuple-element.62), channel_id=1, source_target_pairs={{0,1},{1,2},{2,3},{3,4},{4,5},{5,6},{6,7},{7,8},{8,9},{9,10},{10,1... | collective-permute-start | bytes 30728 | tf_op jit(solution)/shard_map/ppermute | solution.py:18
  304.1 5.4 %collective-permute-start.39 = (f32[5,4,1,128]{3,0,2,1:T(8,128)S(1)}, f32[5,4,1,128]{3,0,2,1:T(8,128)S(1)}, u32[]{:S(2)}, u32[]{:S(2)}) collective-permute-start(f32[5,4,1,128]{3,0,2,1:T(8,128)S(1)} %get-tuple-element.63), channel_id=1, source_target_pairs={{1,0},{2,1},{3,2},{4,3},{5,4},{6,5},{7,6},{8,7},{9,8},{10,9},{11,1... | collective-permute-start | bytes 30728 | tf_op jit(solution)/shard_map/ppermute | solution.py:21
  317.4 8.0 %collective-permute-start.42 = (f32[5,3,1,128]{3,0,2,1:T(8,128)S(1)}, f32[5,3,1,128]{3,0,2,1:T(8,128)S(1)}, u32[]{:S(2)}, u32[]{:S(2)}) collective-permute-start(f32[5,3,1,128]{3,0,2,1:T(8,128)S(1)} %get-tuple-element.76), channel_id=1, source_target_pairs={{0,1},{1,2},{2,3},{3,4},{4,5},{5,6},{6,7},{7,8},{8,9},{9,10},{10,1... | collective-permute-start | bytes 23048 | tf_op jit(solution)/shard_map/ppermute | solution.py:18
  338.9 10.2 %collective-permute-start.46 = (f32[5,3,1,128]{3,0,2,1:T(8,128)S(1)}, f32[5,3,1,128]{3,0,2,1:T(8,128)S(1)}, u32[]{:S(2)}, u32[]{:S(2)}) collective-permute-start(f32[5,3,1,128]{3,0,2,1:T(8,128)S(1)} %get-tuple-element.74), channel_id=1, source_target_pairs={{0,1},{1,2},{2,3},{3,4},{4,5},{5,6},{6,7},{7,8},{8,9},{9,10},{10,1... | collective-permute-start | bytes 23048 | tf_op jit(solution)/shard_map/ppermute | solution.py:18
  342.3 6.8 %collective-permute-start.47 = (f32[5,3,1,128]{3,0,2,1:T(8,128)S(1)}, f32[5,3,1,128]{3,0,2,1:T(8,128)S(1)}, u32[]{:S(2)}, u32[]{:S(2)}) collective-permute-start(f32[5,3,1,128]{3,0,2,1:T(8,128)S(1)} %get-tuple-element.75), channel_id=1, source_target_pairs={{1,0},{2,1},{3,2},{4,3},{5,4},{6,5},{7,6},{8,7},{9,8},{10,9},{11,1... | collective-permute-start | bytes 23048 | tf_op jit(solution)/shard_map/ppermute | solution.py:21
  (22 other events, 137.4 us)
where the time goes:
time: 359 us; the launch traced here: 355 us
  starting transfers between devices  154 us (43%)
  matrix products  140 us (39%)
  waiting for transfers between devices  42.5 us (12%)
  local copies, waits for them, and re-layouts  7.71 us (2%)
  other arithmetic  7.62 us (2%)
    dot_general x243, matrix products, operate(): jnp.einsum('ab,bxyz->axyz', stencil[offset], shifted, precision=lax.Preci...  140 us
    ppermute x24, starting transfers between devices, with_halo(): lax.ppermute(lax.slice_in_dim(block, 0, width, axis=dim), axis, backward)  82.5 us
    ppermute x24, starting transfers between devices, with_halo(): lax.ppermute(lax.slice_in_dim(block, block.shape[dim] - width, None, axis...  71.2 us
    ppermute x24, waiting for transfers between devices, with_halo(): lax.ppermute(lax.slice_in_dim(block, 0, width, axis=dim), axis, backward)  42.4 us
  transfers between devices with their start and end apart: 48, of which 19 were waited for; matrix products, arithmetic and copies ran while one was open for 5% of the time, Pallas kernels for 0%

commit v1 on v0

v1 whole, which is shorter than its diff:
```python
import jax
import jax.numpy as jnp
from jax import lax
from jax.sharding import PartitionSpec as P

COMP = 5
DAMPING = 0.7
WEIGHTS = (0.125, 0.375, 0.375, 0.125)


def exchange(block, hx, hy):
    x_size, y_size = block.shape[1], block.shape[2]
    nx, ny = lax.axis_size("gx"), lax.axis_size("gy")
    kx, ky = -(-hx // x_size), -(-hy // y_size)
    rows = []
    for dx in range(-kx, kx + 1):
        xlo, xhi = max(0, -hx - dx * x_size), min(x_size, x_size + hx - dx * x_size)
        row = []
        for dy in range(-ky, ky + 1):
            ylo, yhi = max(0, -hy - dy * y_size), min(y_size, y_size + hy - dy * y_size)
            piece = block[:, xlo:xhi, ylo:yhi]
            if dx or dy:
                pairs = [
                    ((i + dx) * ny + (j + dy), i * ny + j)
                    for i in range(nx)
                    for j in range(ny)
                    if 0 <= i + dx < nx and 0 <= j + dy < ny
                ]
                piece = lax.ppermute(piece, ("gx", "gy"), pairs)
            row.append(piece)
        rows.append(jnp.concatenate(row, axis=2))
    return jnp.concatenate(rows, axis=1)


def with_halo(block):
    for axis, dim in (("gx", 1), ("gy", 2)):
        count = lax.axis_size(axis)
        forward = [(i, i + 1) for i in range(count - 1)]
        backward = [(target, source) for source, target in forward]
        low = lax.ppermute(lax.slice_in_dim(block, block.shape[dim] - 1, None, axis=dim), axis, forward)
        high = lax.ppermute(lax.slice_in_dim(block, 0, 1, axis=dim), axis, backward)
        block = jnp.concatenate([low, block, high], axis=dim)
    return block


def operate_block(iterate, conduct, rock, stencil):
    masked = rock[None] * iterate
    summed = stencil_sum(with_halo(masked), stencil)
    return conduct * rock[None] * summed


def smooth_block(forcing, conduct, rock, stencil, sweeps):
    diagonal = conduct * jnp.diagonal(stencil[13])[:, None, None, None]
    source = rock[None] * forcing
    iterate = DAMPING * source / diagonal
    for _ in range(sweeps - 1):
        iterate = iterate + DAMPING * (source - operate_block(iterate, conduct, rock, stencil)) / diagonal
    residual = source - operate_block(iterate, conduct, rock, stencil)
    return iterate, residual


def crop(values, h):
    if h == 0:
        return values
    return values[:, h:-h, h:-h]


def stencil_sum(masked, stencil):
    padded = jnp.pad(masked, ((0, 0), (0, 0), (0, 0), (1, 1)))
    ex, ey, ez = masked.shape[1] - 2, masked.shape[2] - 2, masked.shape[3]
    acc = [None] * COMP
    for offset in range(27):
        sx, sy, sz = offset // 9, offset // 3 % 3, offset % 3
        shifted = padded[:, sx : sx + ex, sy : sy + ey, sz : sz + ez]
        for a in range(COMP):
            for b in range(COMP):
                term = stencil[offset, a, b] * shifted[b]
                acc[a] = term if acc[a] is None else acc[a] + term
    return jnp.stack(acc)


def level_chain(iterate, forcing, conduct, rock, stencil, h, sweeps):
    safe = jnp.where(conduct == 0.0, 1.0, conduct)
    diag = jnp.diagonal(stencil[13])[:, None, None, None]
    diagonal = safe * diag
    source = rock[None] * forcing
    if iterate is None:
        iterate = DAMPING * source / diagonal
        remaining = sweeps - 1
    else:
        remaining = sweeps
    for _ in range(remaining):
        masked = rock[None] * iterate
        inner = crop(safe, 1)
        applied = inner * crop_rock(rock)[None] * stencil_sum(masked, stencil)
        iterate = crop(iterate, 1) + DAMPING * (crop(source, 1) - applied) / crop(diagonal, 1)
        safe, diagonal, source, rock = inner, crop(diagonal, 1), crop(source, 1), crop_rock(rock)
    masked = rock[None] * iterate
    inner = crop(safe, 1)
    applied = inner * crop_rock(rock)[None] * stencil_sum(masked, stencil)
    residual = crop(source, 1) - applied
    return iterate, residual


def crop_rock(rock):
    return rock[1:-1, 1:-1]


def shrink(padded):
    extent_x = padded.shape[1] - 2
    along_x = sum(
        WEIGHTS[w] * padded[:, w : w + extent_x - 1 : 2] for w in range(4)
    )
    extent_y = padded.shape[2] - 2
    return sum(WEIGHTS[w] * along_x[:, :, w : w + extent_y - 1 : 2] for w in range(4))


def coarsen(values):
    leading = values.shape[:-3]
    ex, ey, ez = values.shape[-3], values.shape[-2], values.shape[-1]
    reshaped = values.reshape(leading + (ex // 2, 2, ey // 2, 2, ez))
    return reshaped.mean(axis=(-4, -2))


def body(initial_guess, right_side, coefficients, tunnel_mask, stencil):
    rock = tunnel_mask.astype(jnp.float32)
    conduct = coefficients
    h0 = 4
    packed = jnp.concatenate([initial_guess, right_side, conduct, rock[None]], axis=0)
    padded = exchange(packed, h0, h0)
    v_p, f_p, c_p, s_p = padded[0:5], padded[5:10], padded[10:15], padded[15]
    iterate, residual = level_chain(v_p, f_p, c_p, s_p, stencil, h0, 2)
    kept = [crop(iterate, 2)]
    forcing = shrink(residual)
    halos = (3, 3)
    for level in range(2):
        conduct = coarsen(conduct)
        rock = coarsen(rock)
        h = halos[level]
        packed = jnp.concatenate([forcing, conduct, rock[None]], axis=0)
        padded = exchange(packed, h, h)
        f_p, c_p, s_p = padded[0:5], padded[5:10], padded[10]
        iterate, residual = level_chain(None, f_p, c_p, s_p, stencil, h, 2)
        kept.append(crop(iterate, h - 1))
        forcing = shrink(residual)
    conduct = coarsen(conduct)
    rock = coarsen(rock)
    iterate, residual = smooth_block(forcing, conduct, rock, stencil, 2)
    kept.append(residual)
    return tuple(kept)


def solution(mesh):
    placed = (
        P(None, "gx", "gy", None),
        P(None, "gx", "gy", None),
        P(None, "gx", "gy", None),
        P("gx", "gy", None),
        P(),
    )
    return jax.shard_map(
        body,
        mesh=mesh,
        in_specs=placed,
        out_specs=(
            P(None, "gx", "gy", None),
            P(None, "gx", "gy", None),
            P(None, "gx", "gy", None),
            P(None, "gx", "gy", None),
        ),
        check_vma=False,
    )
```

time: 359 us -> 4180 us (11.64); the launches traced: 355 us -> 4120 us
  other arithmetic: 7.62 us -> 3940 us
  matrix products: 140 us -> 0 us
    unnamed x0 -> x40, other arithmetic: none -> 3130 us
    another operation x0 -> x9, other arithmetic: none -> 789 us  [stencil_sum(): return jnp.stack(acc)]
    dot_general x243 -> x0, matrix products: 140 us -> none  [operate(): jnp.einsum('ab,bxyz->axyz', stencil[offset], shifted, precision=lax.Preci...]
    ppermute x48 -> x38, starting transfers between devices: 154 us -> 131 us  [the longest x30 103 us: exchange(): piece = lax.ppermute(piece, ('gx', 'gy'), pairs)]
  transfers between devices with their start and end apart: 48 -> 38, of which waited for: 19 -> 8; matrix products, arithmetic and copies ran while one was open for 5% -> 1% of each run, Pallas kernels for 0% -> 0%
where the time goes in v1:
time: 4180 us; the launch traced here: 4120 us
  other arithmetic  3940 us (94%)
  starting transfers between devices  131 us (3%)
    unnamed x40, other arithmetic  3130 us
    another operation x9, other arithmetic, stencil_sum(): return jnp.stack(acc)  789 us
    ppermute x30, starting transfers between devices, exchange(): piece = lax.ppermute(piece, ('gx', 'gy'), pairs)  103 us
  transfers between devices with their start and end apart: 38, of which 8 were waited for; matrix products, arithmetic and copies ran while one was open for 1% of the time, Pallas kernels for 0%

profile of v1, /device:TPU:41, one launch (start us, length us, event | category | flops | bytes accessed | tf_op | source)
XLA Modules:
  0.0 4122.2 jit_solution(15076830068890930655)
XLA Ops:
  73.6 92.0 %bitcast_dynamic-update-slice_fusion.4 = f32[5,14,38,128]{3,2,1,0:T(8,128)} fusion(f32[1,14,38,128]{3,2,1,0:T(8,128)S(1)} %get-tuple-element.98, f32[1,14,38,128]{3,2,1,0:T(8,128)S(1)} %get-tuple-element.104, f32[1,14,38,128]{3,2,1,0:T(8,128)S(1)} %get-tuple-element.103, f32[1,14,38,128]{3,2,1,0:T(8,128)S(1)} %get-tuple-element.102, ...), kind=kLoop, calls=%fused_computation.1164 | loop fusion | flops 18317824 | bytes 19989020
  165.6 91.2 %bitcast_dynamic-update-slice_fusion.3 = f32[5,14,38,128]{3,2,1,0:T(8,128)} fusion(f32[5,14,38,128]{3,2,1,0:T(8,128)} %bitcast_dynamic-update-slice_fusion.4, f32[1,14,38,128]{3,2,1,0:T(8,128)S(1)} %get-tuple-element.98, f32[1,14,38,128]{3,2,1,0:T(8,128)S(1)} %get-tuple-element.104, f32[1,14,38,128]{3,2,1,0:T(8,128)S(1)} %get-tuple-element.103, ...), kind=kLoop, calls=%fused_computation.1044 | loop fusion | flops 18317824 | bytes 19770880
  256.8 91.4 %bitcast_dynamic-update-slice_fusion.2 = f32[5,14,38,128]{3,2,1,0:T(8,128)} fusion(f32[5,14,38,128]{3,2,1,0:T(8,128)} %bitcast_dynamic-update-slice_fusion.3, f32[1,14,38,128]{3,2,1,0:T(8,128)S(1)} %get-tuple-element.98, f32[1,14,38,128]{3,2,1,0:T(8,128)S(1)} %get-tuple-element.104, f32[1,14,38,128]{3,2,1,0:T(8,128)S(1)} %get-tuple-element.103, ...), kind=kLoop, calls=%fused_computation.924 | loop fusion | flops 18317824 | bytes 19770880
  348.2 91.2 %bitcast_dynamic-update-slice_fusion.1 = f32[5,14,38,128]{3,2,1,0:T(8,128)} fusion(f32[5,14,38,128]{3,2,1,0:T(8,128)} %bitcast_dynamic-update-slice_fusion.2, f32[1,14,38,128]{3,2,1,0:T(8,128)S(1)} %get-tuple-element.98, f32[1,14,38,128]{3,2,1,0:T(8,128)S(1)} %get-tuple-element.104, f32[1,14,38,128]{3,2,1,0:T(8,128)S(1)} %get-tuple-element.103, ...), kind=kLoop, calls=%fused_computation.804 | loop fusion | flops 18317824 | bytes 19770880
  439.3 92.3 %bitcast_dynamic-update-slice_fusion = f32[5,14,38,128]{3,2,1,0:T(8,128)} fusion(f32[5,14,38,128]{3,2,1,0:T(8,128)} %bitcast_dynamic-update-slice_fusion.1, f32[1,14,38,128]{3,2,1,0:T(8,128)S(1)} %get-tuple-element.98, f32[1,14,38,128]{3,2,1,0:T(8,128)S(1)} %get-tuple-element.104, f32[1,14,38,128]{3,2,1,0:T(8,128)S(1)} %get-tuple-element.103, ...), kind=kLoop, calls=%fused_computation.684 | loop fusion | flops 18317824 | bytes 19770880 | tf_op jit(solution)/shard_map/stack | solution.py:79
  533.8 91.5 %bitcast_dynamic-update-slice_fusion.9 = f32[5,12,36,128]{3,2,1,0:T(8,128)S(1)} fusion(f32[5,14,38,128]{3,2,1,0:T(8,128)S(1)} %get-tuple-element.83, f32[]{:T(128)} %bitcast.255, f32[]{:T(128)} %bitcast.253, f32[]{:T(128)} %bitcast.251, f32[]{:T(128)} %bitcast.249, f32[]{:T(128)} %bitcast.247, f32[]{:T(128)} %bitcast.245, f32[]{:T(128)} %bitcast.243, ...), kind=kLoop, calls=%fused_computation.1777 | loop fusion | flops 14874623 | bytes 12739100
  625.3 90.5 %bitcast_dynamic-update-slice_fusion.8 = f32[5,12,36,128]{3,2,1,0:T(8,128)S(1)} fusion(f32[5,12,36,128]{3,2,1,0:T(8,128)S(1)} %bitcast_dynamic-update-slice_fusion.9, f32[5,14,38,128]{3,2,1,0:T(8,128)S(1)} %get-tuple-element.83, f32[]{:T(128)} %bitcast.511, f32[]{:T(128)} %bitcast.509, f32[]{:T(128)} %bitcast.507, f32[]{:T(128)} %bitcast.505, ...), kind=kLoop, calls=%fused_computation.1657 | loop fusion | flops 14874624 | bytes 12739100
  715.8 91.3 %bitcast_dynamic-update-slice_fusion.7 = f32[5,12,36,128]{3,2,1,0:T(8,128)S(1)} fusion(f32[5,12,36,128]{3,2,1,0:T(8,128)S(1)} %bitcast_dynamic-update-slice_fusion.8, f32[5,14,38,128]{3,2,1,0:T(8,128)S(1)} %get-tuple-element.83, f32[]{:T(128)} %bitcast.767, f32[]{:T(128)} %bitcast.765, f32[]{:T(128)} %bitcast.763, f32[]{:T(128)} %bitcast.761, ...), kind=kLoop, calls=%fused_computation.1537 | loop fusion | flops 14874624 | bytes 12739100
  807.1 90.6 %bitcast_dynamic-update-slice_fusion.6 = f32[5,12,36,128]{3,2,1,0:T(8,128)S(1)} fusion(f32[5,12,36,128]{3,2,1,0:T(8,128)S(1)} %bitcast_dynamic-update-slice_fusion.7, f32[5,14,38,128]{3,2,1,0:T(8,128)S(1)} %get-tuple-element.83, f32[]{:T(128)} %bitcast.1023, f32[]{:T(128)} %bitcast.1021, f32[]{:T(128)} %bitcast.1019, f32[]{:T(128)} %bitcast.1017, ...), kind=kLoop, calls=%fused_computation.1417 | loop fusion | flops 14874624 | bytes 12739100
  897.7 91.5 %bitcast_dynamic-update-slice_fusion.5 = f32[5,12,36,128]{3,2,1,0:T(8,128)S(1)} fusion(f32[5,12,36,128]{3,2,1,0:T(8,128)S(1)} %bitcast_dynamic-update-slice_fusion.6, f32[5,14,38,128]{3,2,1,0:T(8,128)S(1)} %get-tuple-element.83, f32[]{:T(128)} %bitcast.1279, f32[]{:T(128)} %bitcast.1277, f32[]{:T(128)} %bitcast.1275, f32[]{:T(128)} %bitcast.1273, ...), kind=kLoop, calls=%fused_computation.1297 | loop fusion | flops 14874624 | bytes 12739100 | tf_op jit(solution)/shard_map/stack | solution.py:79
  990.9 89.8 %bitcast_dynamic-update-slice_fusion.14 = f32[5,10,34,128]{3,2,1,0:T(8,128)S(1)} fusion(f32[1,10,34,128]{3,2,1,0:T(8,128)S(1)} %get-tuple-element.116, f32[1,10,34,128]{3,2,1,0:T(8,128)S(1)} %get-tuple-element.122, f32[1,10,34,128]{3,2,1,0:T(8,128)S(1)} %get-tuple-element.121, f32[1,10,34,128]{3,2,1,0:T(8,128)S(1)} %get-tuple-element.120, ...), kind=kLoop, calls=%fused_computation.2408 | loop fusion | flops 11706879 | bytes 14336540
  1080.8 88.5 %bitcast_dynamic-update-slice_fusion.13 = f32[5,10,34,128]{3,2,1,0:T(8,128)S(1)} fusion(f32[5,10,34,128]{3,2,1,0:T(8,128)S(1)} %bitcast_dynamic-update-slice_fusion.14, f32[1,10,34,128]{3,2,1,0:T(8,128)S(1)} %get-tuple-element.116, f32[1,10,34,128]{3,2,1,0:T(8,128)S(1)} %get-tuple-element.122, f32[1,10,34,128]{3,2,1,0:T(8,128)S(1)} %get-tuple-element.121, ...), kind=kLoop, calls=%fused_computation.2288 | loop fusion | flops 11706880 | bytes 14131740
  1169.3 88.8 %bitcast_dynamic-update-slice_fusion.12 = f32[5,10,34,128]{3,2,1,0:T(8,128)S(1)} fusion(f32[5,10,34,128]{3,2,1,0:T(8,128)S(1)} %bitcast_dynamic-update-slice_fusion.13, f32[1,10,34,128]{3,2,1,0:T(8,128)S(1)} %get-tuple-element.116, f32[1,10,34,128]{3,2,1,0:T(8,128)S(1)} %get-tuple-element.122, f32[1,10,34,128]{3,2,1,0:T(8,128)S(1)} %get-tuple-element.121, ...), kind=kLoop, calls=%fused_computation.2168 | loop fusion | flops 11706880 | bytes 14131740
  1258.2 88.7 %bitcast_dynamic-update-slice_fusion.11 = f32[5,10,34,128]{3,2,1,0:T(8,128)S(1)} fusion(f32[5,10,34,128]{3,2,1,0:T(8,128)S(1)} %bitcast_dynamic-update-slice_fusion.12, f32[1,10,34,128]{3,2,1,0:T(8,128)S(1)} %get-tuple-element.116, f32[1,10,34,128]{3,2,1,0:T(8,128)S(1)} %get-tuple-element.122, f32[1,10,34,128]{3,2,1,0:T(8,128)S(1)} %get-tuple-element.121, ...), kind=kLoop, calls=%fused_computation.2048 | loop fusion | flops 11706880 | bytes 14131740
  1346.8 89.5 %bitcast_dynamic-update-slice_fusion.10 = f32[5,10,34,128]{3,2,1,0:T(8,128)S(1)} fusion(f32[5,10,34,128]{3,2,1,0:T(8,128)S(1)} %bitcast_dynamic-update-slice_fusion.11, f32[1,10,34,128]{3,2,1,0:T(8,128)S(1)} %get-tuple-element.116, f32[1,10,34,128]{3,2,1,0:T(8,128)S(1)} %get-tuple-element.122, f32[1,10,34,128]{3,2,1,0:T(8,128)S(1)} %get-tuple-element.121, ...), kind=kLoop, calls=%fused_computation.1928 | loop fusion | flops 11706880 | bytes 14131740 | tf_op jit(solution)/shard_map/stack | solution.py:79
  1471.0 87.5 %constant_dynamic-update-slice_fusion.4 = f32[5,8,20,128]{3,2,1,0:T(8,128)S(1)} fusion(f32[5,10,22,128]{3,2,1,0:T(8,128)S(1)} %get-tuple-element.76, f32[]{:T(128)} %bitcast.255, f32[]{:T(128)} %bitcast.253, f32[]{:T(128)} %bitcast.251, f32[]{:T(128)} %bitcast.249, f32[]{:T(128)} %bitcast.247, f32[]{:T(128)} %bitcast.245, f32[]{:T(128)} %bitcast.243, ...), kind=kLoop, calls=%fused_computation.2672 | loop fusion | flops 5509119 | bytes 5136924
  1558.5 86.3 %constant_dynamic-update-slice_fusion.3 = f32[5,8,20,128]{3,2,1,0:T(8,128)S(1)} fusion(f32[5,8,20,128]{3,2,1,0:T(8,128)S(1)} %constant_dynamic-update-slice_fusion.4, f32[5,10,22,128]{3,2,1,0:T(8,128)S(1)} %get-tuple-element.76, f32[]{:T(128)} %bitcast.511, f32[]{:T(128)} %bitcast.509, f32[]{:T(128)} %bitcast.507, f32[]{:T(128)} %bitcast.505, ...), kind=kLoop, calls=%fused_computation.2671 | loop fusion | flops 5509120 | bytes 5136924
  1644.8 86.6 %constant_dynamic-update-slice_fusion.2 = f32[5,8,20,128]{3,2,1,0:T(8,128)S(1)} fusion(f32[5,8,20,128]{3,2,1,0:T(8,128)S(1)} %constant_dynamic-update-slice_fusion.3, f32[5,10,22,128]{3,2,1,0:T(8,128)S(1)} %get-tuple-element.76, f32[]{:T(128)} %bitcast.767, f32[]{:T(128)} %bitcast.765, f32[]{:T(128)} %bitcast.763, f32[]{:T(128)} %bitcast.761, ...), kind=kLoop, calls=%fused_computation.2670 | loop fusion | flops 5509120 | bytes 5136924
  1731.4 86.6 %constant_dynamic-update-slice_fusion.1 = f32[5,8,20,128]{3,2,1,0:T(8,128)S(1)} fusion(f32[5,8,20,128]{3,2,1,0:T(8,128)S(1)} %constant_dynamic-update-slice_fusion.2, f32[5,10,22,128]{3,2,1,0:T(8,128)S(1)} %get-tuple-element.76, f32[]{:T(128)} %bitcast.1023, f32[]{:T(128)} %bitcast.1021, f32[]{:T(128)} %bitcast.1019, f32[]{:T(128)} %bitcast.1017, ...), kind=kLoop, calls=%fused_computation.2669 | loop fusion | flops 5509120 | bytes 5136924
  1817.9 87.3 %constant_dynamic-update-slice_fusion = f32[5,8,20,128]{3,2,1,0:T(8,128)S(1)} fusion(f32[5,8,20,128]{3,2,1,0:T(8,128)S(1)} %constant_dynamic-update-slice_fusion.1, f32[5,10,22,128]{3,2,1,0:T(8,128)S(1)} %get-tuple-element.76, f32[]{:T(128)} %bitcast.1279, f32[]{:T(128)} %bitcast.1277, f32[]{:T(128)} %bitcast.1275, f32[]{:T(128)} %bitcast.1273, ...), kind=kLoop, calls=%fused_computation.2668 | loop fusion | flops 5509120 | bytes 5136924 | tf_op jit(solution)/shard_map/stack | solution.py:79
  1905.6 86.9 %constant_dynamic-update-slice_fusion.9 = f32[5,6,18,128]{3,2,1,0:T(8,128)S(1)} fusion(f32[5,8,20,128]{3,2,1,0:T(8,128)S(1)} %get-tuple-element.74, f32[]{:T(128)} %bitcast.255, f32[]{:T(128)} %bitcast.253, f32[]{:T(128)} %bitcast.251, f32[]{:T(128)} %bitcast.249, f32[]{:T(128)} %bitcast.247, f32[]{:T(128)} %bitcast.245, f32[]{:T(128)} %bitcast.243, ...), kind=kLoop, calls=%fused_computation.2677 | loop fusion | flops 3718655 | bytes 3883548
  1992.5 85.6 %constant_dynamic-update-slice_fusion.8 = f32[5,6,18,128]{3,2,1,0:T(8,128)S(1)} fusion(f32[5,6,18,128]{3,2,1,0:T(8,128)S(1)} %constant_dynamic-update-slice_fusion.9, f32[5,8,20,128]{3,2,1,0:T(8,128)S(1)} %get-tuple-element.74, f32[]{:T(128)} %bitcast.511, f32[]{:T(128)} %bitcast.509, f32[]{:T(128)} %bitcast.507, f32[]{:T(128)} %bitcast.505, f32[]{:T(128)} %bitcast.503, ...), kind=kLoop, calls=%fused_computation.2676 | loop fusion | flops 3718656 | bytes 3883548
  2078.1 86.1 %constant_dynamic-update-slice_fusion.7 = f32[5,6,18,128]{3,2,1,0:T(8,128)S(1)} fusion(f32[5,6,18,128]{3,2,1,0:T(8,128)S(1)} %constant_dynamic-update-slice_fusion.8, f32[5,8,20,128]{3,2,1,0:T(8,128)S(1)} %get-tuple-element.74, f32[]{:T(128)} %bitcast.767, f32[]{:T(128)} %bitcast.765, f32[]{:T(128)} %bitcast.763, f32[]{:T(128)} %bitcast.761, f32[]{:T(128)} %bitcast.759, ...), kind=kLoop, calls=%fused_computation.2675 | loop fusion | flops 3718656 | bytes 3883548
  2164.3 85.7 %constant_dynamic-update-slice_fusion.6 = f32[5,6,18,128]{3,2,1,0:T(8,128)S(1)} fusion(f32[5,6,18,128]{3,2,1,0:T(8,128)S(1)} %constant_dynamic-update-slice_fusion.7, f32[5,8,20,128]{3,2,1,0:T(8,128)S(1)} %get-tuple-element.74, f32[]{:T(128)} %bitcast.1023, f32[]{:T(128)} %bitcast.1021, f32[]{:T(128)} %bitcast.1019, f32[]{:T(128)} %bitcast.1017, ...), kind=kLoop, calls=%fused_computation.2674 | loop fusion | flops 3718656 | bytes 3883548
  2250.0 86.6 %constant_dynamic-update-slice_fusion.5 = f32[5,6,18,128]{3,2,1,0:T(8,128)S(1)} fusion(f32[5,6,18,128]{3,2,1,0:T(8,128)S(1)} %constant_dynamic-update-slice_fusion.6, f32[5,8,20,128]{3,2,1,0:T(8,128)S(1)} %get-tuple-element.74, f32[]{:T(128)} %bitcast.1279, f32[]{:T(128)} %bitcast.1277, f32[]{:T(128)} %bitcast.1275, f32[]{:T(128)} %bitcast.1273, ...), kind=kLoop, calls=%fused_computation.2673 | loop fusion | flops 3718656 | bytes 3883548 | tf_op jit(solution)/shard_map/stack | solution.py:79
  2385.4 86.3 %constant_dynamic-update-slice_fusion.16 = f32[5,6,12,128]{3,2,1,0:T(8,128)S(1)} fusion(f32[5,8,14,128]{3,2,1,0:T(8,128)S(1)} %get-tuple-element.70, f32[]{:T(128)} %bitcast.255, f32[]{:T(128)} %bitcast.253, f32[]{:T(128)} %bitcast.251, f32[]{:T(128)} %bitcast.249, f32[]{:T(128)} %bitcast.247, f32[]{:T(128)} %bitcast.245, f32[]{:T(128)} %bitcast.243, ...), kind=kLoop, calls=%fused_computation.2684 | loop fusion | flops 2479103 | bytes 2589212
  2556.6 85.2 %constant_dynamic-update-slice_fusion.14 = f32[5,6,12,128]{3,2,1,0:T(8,128)S(1)} fusion(f32[5,6,12,128]{3,2,1,0:T(8,128)S(1)} %constant_dynamic-update-slice_fusion.15, f32[5,8,14,128]{3,2,1,0:T(8,128)S(1)} %get-tuple-element.70, f32[]{:T(128)} %bitcast.767, f32[]{:T(128)} %bitcast.765, f32[]{:T(128)} %bitcast.763, f32[]{:T(128)} %bitcast.761, ...), kind=kLoop, calls=%fused_computation.2682 | loop fusion | flops 2479104 | bytes 2589212
  2726.9 85.9 %constant_dynamic-update-slice_fusion.12 = f32[5,6,12,128]{3,2,1,0:T(8,128)S(1)} fusion(f32[5,6,12,128]{3,2,1,0:T(8,128)S(1)} %constant_dynamic-update-slice_fusion.13, f32[5,8,14,128]{3,2,1,0:T(8,128)S(1)} %get-tuple-element.70, f32[]{:T(128)} %bitcast.1279, f32[]{:T(128)} %bitcast.1277, f32[]{:T(128)} %bitcast.1275, f32[]{:T(128)} %bitcast.1273, ...), kind=kLoop, calls=%fused_computation.2680 | loop fusion | flops 2479104 | bytes 2589212 | tf_op jit(solution)/shard_map/stack | solution.py:79
  2813.0 86.1 %constant_dynamic-update-slice_fusion.21 = f32[5,4,10,128]{3,2,1,0:T(8,128)S(1)} fusion(f32[5,6,12,128]{3,2,1,0:T(8,128)S(1)} %get-tuple-element.68, f32[]{:T(128)} %bitcast.255, f32[]{:T(128)} %bitcast.253, f32[]{:T(128)} %bitcast.251, f32[]{:T(128)} %bitcast.249, f32[]{:T(128)} %bitcast.247, f32[]{:T(128)} %bitcast.245, f32[]{:T(128)} %bitcast.243, ...), kind=kLoop, calls=%fused_computation.2689 | loop fusion | flops 1377279 | bytes 1753628
  3152.9 85.5 %constant_dynamic-update-slice_fusion.17 = f32[5,4,10,128]{3,2,1,0:T(8,128)S(1)} fusion(f32[5,4,10,128]{3,2,1,0:T(8,128)S(1)} %constant_dynamic-update-slice_fusion.18, f32[5,6,12,128]{3,2,1,0:T(8,128)S(1)} %get-tuple-element.68, f32[]{:T(128)} %bitcast.1279, f32[]{:T(128)} %bitcast.1277, f32[]{:T(128)} %bitcast.1275, f32[]{:T(128)} %bitcast.1273, ...), kind=kLoop, calls=%fused_computation.2685 | loop fusion | flops 1377280 | bytes 1753628 | tf_op jit(solution)/shard_map/stack | solution.py:79
  3258.7 85.3 %constant_dynamic-update-slice_fusion.26 = (f32[5,1,4,128]{3,2,1,0:T(4,128)S(1)}, f32[1,1,4,128]{3,2,1,0:T(4,128)S(1)}, f32[1,1,4,128]{3,2,1,0:T(4,128)S(1)}, f3...) fusion(f32[5,3,6,130]{3,2,1,0:T(8,128)S(1)} %select_maximum_fus, ...), kind=kLoop, calls=%fused_computation.2694 | loop fusion | flops 183807 | bytes 325148
  3699.2 85.3 %constant_dynamic-update-slice_fusion.31 = (f32[5,1,4,128]{3,2,1,0:T(4,128)S(1)}, f32[1,1,4,128]{3,2,1,0:T(4,128)S(1)}, f32[1,1,4,128]{3,2,1,0:T(4,128)S(1)}, f3...) fusion(f32[5,3,6,130]{3,2,1,0:T(8,128)S(1)} %select_maximum_fus, ...), kind=kLoop, calls=%fused_computation.2699 | loop fusion | flops 183807 | bytes 325148
  (221 shorter events, 1296.5 us)
Async XLA Ops:
  3.9 45.7 %collective-permute-start = (f32[16,4,4,128]{3,2,1,0:T(4,128)}, f32[16,4,4,128]{3,2,1,0:T(4,128)}, u32[]{:S(2)}, u32[]{:S(2)}) collective-permute-start(f32[16,4,4,128]{3,2,1,0:T(4,128)} %get-tuple-element.89), channel_id=1, source_target_pairs={{0,17},{1,18},{2,19},{3,20},{4,21},{5,22},{6,23},{7,24},{8,25},{9,... | collective-permute-start | bytes 393224 | tf_op jit(solution)/shard_map/ppermute | solution.py:29
  8.9 42.6 %collective-permute-start.2 = (f32[16,4,4,128]{3,2,1,0:T(4,128)}, f32[16,4,4,128]{3,2,1,0:T(4,128)}, u32[]{:S(2)}, u32[]{:S(2)}) collective-permute-start(f32[16,4,4,128]{3,2,1,0:T(4,128)} %get-tuple-element.92), channel_id=1, source_target_pairs={{1,16},{2,17},{3,18},{4,19},{5,20},{6,21},{7,22},{8,23},{9,24},{10... | collective-permute-start | bytes 393224 | tf_op jit(solution)/shard_map/ppermute | solution.py:29
  12.9 44.8 %collective-permute-start.5 = (f32[16,4,4,128]{3,2,1,0:T(4,128)}, f32[16,4,4,128]{3,2,1,0:T(4,128)}, u32[]{:S(2)}, u32[]{:S(2)}) collective-permute-start(f32[16,4,4,128]{3,2,1,0:T(4,128)} %get-tuple-element.91), channel_id=1, source_target_pairs={{16,1},{17,2},{18,3},{19,4},{20,5},{21,6},{22,7},{23,8},{24,9},{25... | collective-permute-start | bytes 393224 | tf_op jit(solution)/shard_map/ppermute | solution.py:29
  16.6 49.5 %collective-permute-start.1 = (f32[16,4,32,128]{3,2,1,0:T(8,128)}, f32[16,4,32,128]{3,2,1,0:T(8,128)S(1)}, u32[]{:S(2)}, u32[]{:S(2)}) collective-permute-start(f32[16,4,32,128]{3,2,1,0:T(8,128)} %get-tuple-element.93), channel_id=1, source_target_pairs={{0,16},{1,17},{2,18},{3,19},{4,20},{5,21},{6,22},{7,23},{8,24},{9,... | collective-permute-start | bytes 3145736 | tf_op jit(solution)/shard_map/ppermute | solution.py:29
  20.5 45.6 %collective-permute-start.6 = (f32[16,4,32,128]{3,2,1,0:T(8,128)}, f32[16,4,32,128]{3,2,1,0:T(8,128)}, u32[]{:S(2)}, u32[]{:S(2)}) collective-permute-start(f32[16,4,32,128]{3,2,1,0:T(8,128)} %get-tuple-element.94), channel_id=1, source_target_pairs={{16,0},{17,1},{18,2},{19,3},{20,4},{21,5},{22,6},{23,7},{24,8},{25... | collective-permute-start | bytes 3145736 | tf_op jit(solution)/shard_map/ppermute | solution.py:29
  49.6 16.5 collective-permute-start.3
  51.6 14.5 collective-permute-start.4
  57.8 8.3 collective-permute-start.7
  1437.8 32.8 collective-permute-start.14
  1440.3 30.3 collective-permute-start.9
  1443.3 14.5 collective-permute-start.10
  1449.7 10.1 collective-permute-start.13
  1451.6 10.1 collective-permute-start.15
  1457.8 11.0 collective-permute-start.8
  1459.8 9.7 collective-permute-start.11
  1461.7 8.8 collective-permute-start.12
  2337.4 21.9 collective-permute-start.17
  2340.5 11.8 collective-permute-start.16
  2343.2 11.9 collective-permute-start.18
  2348.5 23.9 collective-permute-start.20
  2350.4 11.3 collective-permute-start.19
  2352.3 23.1 collective-permute-start.22
  2355.1 10.6 collective-permute-start.21
  2359.3 18.1 collective-permute-start.23
  2361.7 17.7 collective-permute-start.24
  2365.7 16.1 collective-permute-start.26
  2372.3 9.4 collective-permute-start.25
  2375.5 9.7 collective-permute-start.28
  2377.4 7.7 collective-permute-start.27
  3248.8 9.2 collective-permute-start.32
  3250.7 7.8 collective-permute-start.33
  3688.8 10.2 collective-permute-start.36
  (12 other events, 170.3 us)

commit v2 on v1

--- a/solution.py
+++ b/solution.py
@@ -3,7 +3,6 @@
 from jax import lax
 from jax.sharding import PartitionSpec as P
 
-COMP = 5
 DAMPING = 0.7
 WEIGHTS = (0.125, 0.375, 0.375, 0.125)
 
@@ -49,11 +48,13 @@
     return conduct * rock[None] * summed
 
 
-def smooth_block(forcing, conduct, rock, stencil, sweeps):
+def smooth_block(iterate, forcing, conduct, rock, stencil, sweeps):
     diagonal = conduct * jnp.diagonal(stencil[13])[:, None, None, None]
     source = rock[None] * forcing
-    iterate = DAMPING * source / diagonal
-    for _ in range(sweeps - 1):
+    if iterate is None:
+        iterate = DAMPING * source / diagonal
+        sweeps = sweeps - 1
+    for _ in range(sweeps):
         iterate = iterate + DAMPING * (source - operate_block(iterate, conduct, rock, stencil)) / diagonal
     residual = source - operate_block(iterate, conduct, rock, stencil)
     return iterate, residual
@@ -68,15 +69,14 @@
 def stencil_sum(masked, stencil):
     padded = jnp.pad(masked, ((0, 0), (0, 0), (0, 0), (1, 1)))
     ex, ey, ez = masked.shape[1] - 2, masked.shape[2] - 2, masked.shape[3]
-    acc = [None] * COMP
+    summed = jnp.zeros((masked.shape[0], ex, ey, ez), jnp.float32)
     for offset in range(27):
         sx, sy, sz = offset // 9, offset // 3 % 3, offset % 3
         shifted = padded[:, sx : sx + ex, sy : sy + ey, sz : sz + ez]
-        for a in range(COMP):
-            for b in range(COMP):
-                term = stencil[offset, a, b] * shifted[b]
-                acc[a] = term if acc[a] is None else acc[a] + term
-    return jnp.stack(acc)
+        summed = summed + jnp.einsum(
+            "ab,bxyz->axyz", stencil[offset], shifted, precision=lax.Precision.HIGHEST
+        )
+    return summed
 
 
 def level_chain(iterate, forcing, conduct, rock, stencil, h, sweeps):
@@ -125,13 +125,9 @@
 def body(initial_guess, right_side, coefficients, tunnel_mask, stencil):
     rock = tunnel_mask.astype(jnp.float32)
     conduct = coefficients
-    h0 = 4
-    packed = jnp.concatenate([initial_guess, right_side, conduct, rock[None]], axis=0)
-    padded = exchange(packed, h0, h0)
-    v_p, f_p, c_p, s_p = padded[0:5], padded[5:10], padded[10:15], padded[15]
-    iterate, residual = level_chain(v_p, f_p, c_p, s_p, stencil, h0, 2)
-    kept = [crop(iterate, 2)]
-    forcing = shrink(residual)
+    iterate, residual = smooth_block(initial_guess, right_side, conduct, rock, stencil, 2)
+    kept = [iterate]
+    forcing = shrink(with_halo(residual))
     halos = (3, 3)
     for level in range(2):
         conduct = coarsen(conduct)
@@ -145,7 +141,7 @@
         forcing = shrink(residual)
     conduct = coarsen(conduct)
     rock = coarsen(rock)
-    iterate, residual = smooth_block(forcing, conduct, rock, stencil, 2)
+    iterate, residual = smooth_block(None, forcing, conduct, rock, stencil, 2)
     kept.append(residual)
     return tuple(kept)
 

time: 4180 us -> 367 us (0.09); the launches traced: 4120 us -> 363 us
  other arithmetic: 3940 us -> 7.65 us
  matrix products: 0 us -> 166 us
    unnamed x40 -> x4, other arithmetic: 3130 us -> 0.09 us
    another operation x9 -> x0, other arithmetic: 789 us -> none  [stencil_sum(): return jnp.stack(acc)]
    dot_general x0 -> x243, matrix products: none -> 166 us  [stencil_sum(): jnp.einsum('ab,bxyz->axyz', stencil[offset], shifted, precision=lax.Preci...]
    ppermute x30 -> x22, starting transfers between devices: 103 us -> 74.5 us  [exchange(): piece = lax.ppermute(piece, ('gx', 'gy'), pairs)]
  transfers between devices with their start and end apart: 38 -> 46, of which waited for: 8 -> 11; matrix products, arithmetic and copies ran while one was open for 1% -> 5% of each run, Pallas kernels for 0% -> 0%
where the time goes in v2:
time: 367 us; the launch traced here: 363 us
  matrix products  166 us (45%)
  starting transfers between devices  154 us (42%)
  waiting for transfers between devices  24.4 us (7%)
  local copies, waits for them, and re-layouts  7.92 us (2%)
  other arithmetic  7.65 us (2%)
    dot_general x243, matrix products, stencil_sum(): jnp.einsum('ab,bxyz->axyz', stencil[offset], shifted, precision=lax.Preci...  166 us
    ppermute x22, starting transfers between devices, exchange(): piece = lax.ppermute(piece, ('gx', 'gy'), pairs)  74.5 us
    ppermute x12, starting transfers between devices, with_halo(): high = lax.ppermute(lax.slice_in_dim(block, 0, 1, axis=dim), axis, backward)  43.4 us
    ppermute x12, starting transfers between devices, with_halo(): lax.ppermute(lax.slice_in_dim(block, block.shape[dim] - 1, None, axis=dim...  35.8 us
    ppermute x12, waiting for transfers between devices, with_halo(): high = lax.ppermute(lax.slice_in_dim(block, 0, 1, axis=dim), axis, backward)  18.5 us
  transfers between devices with their start and end apart: 46, of which 11 were waited for; matrix products, arithmetic and copies ran while one was open for 5% of the time, Pallas kernels for 0%

profile of v2, /device:TPU:41, one launch (start us, length us, event | category | flops | bytes accessed | tf_op | source)
XLA Modules:
  0.0 363.0 jit_solution(10240731454019318737)
XLA Ops:
  3.2 4.1 %collective-permute-start = (f32[5,1,32,128]{3,0,2,1:T(8,128)S(1)}, f32[5,1,32,128]{3,0,2,1:T(8,128)S(1)}, u32[]{:S(2)}, u32[]{:S(2)}) collective-permute-start(f32[5,1,32,128]{3,0,2,1:T(8,128)S(1)} %get-tuple-element.49), channel_id=1, source_target_pairs={{0,16},{16,32},{32,48},{48,64},{64,80},{80,96},{96,112},{1,17},{17... | collective-permute-start | bytes 245768 | tf_op jit(solution)/shard_map/ppermute | solution.py:39
  16.4 3.1 collective-permute-start.2
  19.5 4.5 %collective-permute-start.3 = (f32[5,10,1,128]{3,0,2,1:T(8,128)S(1)}, f32[5,10,1,128]{3,0,2,1:T(8,128)S(1)}, u32[]{:S(2)}, u32[]{:S(2)}) collective-permute-start(f32[5,10,1,128]{3,0,2,1:T(8,128)S(1)} %get-tuple-element.42), channel_id=1, source_target_pairs={{1,0},{2,1},{3,2},{4,3},{5,4},{6,5},{7,6},{8,7},{9,8},{10,9},{11,1... | collective-permute-start | bytes 76808 | tf_op jit(solution)/shard_map/ppermute | solution.py:40
  53.4 3.1 broadcast_multiply_fusion.1
  56.6 4.2 %collective-permute-start.4 = (f32[5,1,32,128]{3,0,2,1:T(8,128)S(1)}, f32[5,1,32,128]{3,0,2,1:T(8,128)S(1)}, u32[]{:S(2)}, u32[]{:S(2)}) collective-permute-start(f32[5,1,32,128]{3,0,2,1:T(8,128)S(1)} %get-tuple-element.47), channel_id=1, source_target_pairs={{0,16},{16,32},{32,48},{48,64},{64,80},{80,96},{96,112},{1,17},{17... | collective-permute-start | bytes 245768 | tf_op jit(solution)/shard_map/ppermute | solution.py:39
  63.7 3.3 collective-permute-done.5
  69.2 5.5 %collective-permute-start.7 = (f32[5,10,1,128]{3,0,2,1:T(8,128)S(1)}, f32[5,10,1,128]{3,0,2,1:T(8,128)S(1)}, u32[]{:S(2)}, u32[]{:S(2)}) collective-permute-start(f32[5,10,1,128]{3,0,2,1:T(8,128)S(1)} %get-tuple-element.40), channel_id=1, source_target_pairs={{1,0},{2,1},{3,2},{4,3},{5,4},{6,5},{7,6},{8,7},{9,8},{10,9},{11,1... | collective-permute-start | bytes 76808 | tf_op jit(solution)/shard_map/ppermute | solution.py:40
  103.8 3.7 %broadcast_multiply_fusion = (f32[5,8,32,128]{3,0,2,1:T(8,128)S(1)}, f32[5,8,32,128]{3,0,2,1:T(8,128)}) fusion(f32[8,32,128]{2,1,0:T(8,128)S(1)} %convert_element_type.18, f32[5,8,32,128]{3,0,2,1:T(8,128)S(1)} %get-tuple-element.106, f32[5]{0:T(128)S(1)} %gather_fusion, f32[5,8,32,128]{3,0,2,1:T(8,128)S(1)} %convolution_bitcast_fusion.16, ...), kind=kOutput, calls=%fused_computation.577 | convolution fusion | flops 13434880 | bytes 18485760 | tf_op jit(solution)/shard_map/ab,bxyz->axyz/dot_general | solution.py:76
  113.0 3.3 collective-permute-done.9
  118.6 5.2 %collective-permute-start.11 = (f32[5,10,1,128]{3,0,2,1:T(8,128)S(1)}, f32[5,10,1,128]{3,0,2,1:T(8,128)S(1)}, u32[]{:S(2)}, u32[]{:S(2)}) collective-permute-start(f32[5,10,1,128]{3,0,2,1:T(8,128)S(1)} %get-tuple-element.38), channel_id=1, source_target_pairs={{1,0},{2,1},{3,2},{4,3},{5,4},{6,5},{7,6},{8,7},{9,8},{10,9},{11,1... | collective-permute-start | bytes 76808 | tf_op jit(solution)/shard_map/ppermute | solution.py:40
  160.2 4.3 %collective-permute-done.13 = f32[5,1,32,128]{3,0,2,1:T(8,128)S(1)} collective-permute-done((f32[5,1,32,128]{3,0,2,1:T(8,128)S(1)}, f32[5,1,32,128]{3,0,2,1:T(8,128)S(1)}, u32[]{:S(2)}, u32[]{:S(2)}) %collective-permute-start.13) | collective-permute-done | bytes 81952 | tf_op jit(solution)/shard_map/ppermute | solution.py:40
  166.9 5.0 %collective-permute-start.15 = (f32[5,10,1,128]{3,0,2,1:T(8,128)S(1)}, f32[5,10,1,128]{3,0,2,1:T(8,128)S(1)}, u32[]{:S(2)}, u32[]{:S(2)}) collective-permute-start(f32[5,10,1,128]{3,0,2,1:T(8,128)S(1)} %get-tuple-element.36), channel_id=1, source_target_pairs={{1,0},{2,1},{3,2},{4,3},{5,4},{6,5},{7,6},{8,7},{9,8},{10,9},{11,1... | collective-permute-start | bytes 76808 | tf_op jit(solution)/shard_map/ppermute | solution.py:40
  173.6 2.9 collective-permute-start.17
  178.5 4.5 %collective-permute-start.16 = (f32[11,3,3,128]{3,0,2,1:T(8,128)S(1)}, f32[11,3,3,128]{3,0,2,1:T(8,128)S(1)}, u32[]{:S(2)}, u32[]{:S(2)}) collective-permute-start(f32[11,3,3,128]{3,0,2,1:T(8,128)S(1)} %get-tuple-element.52), channel_id=1, source_target_pairs={{0,17},{1,18},{2,19},{3,20},{4,21},{5,22},{6,23},{7,24},{8,25},{9,... | collective-permute-start | bytes 152072 | tf_op jit(solution)/shard_map/ppermute | solution.py:28
  183.0 4.9 %collective-permute-start.18 = (f32[11,3,3,128]{3,0,2,1:T(8,128)S(1)}, f32[11,3,3,128]{3,0,2,1:T(8,128)S(1)}, u32[]{:S(2)}, u32[]{:S(2)}) collective-permute-start(f32[11,3,3,128]{3,0,2,1:T(8,128)S(1)} %get-tuple-element.55), channel_id=1, source_target_pairs={{1,16},{2,17},{3,18},{4,19},{5,20},{6,21},{7,22},{8,23},{9,24},{10... | collective-permute-start | bytes 152072 | tf_op jit(solution)/shard_map/ppermute | solution.py:28
  189.9 5.3 %collective-permute-start.23 = (f32[11,3,3,128]{3,0,2,1:T(8,128)S(1)}, f32[11,3,3,128]{3,0,2,1:T(8,128)S(1)}, u32[]{:S(2)}, u32[]{:S(2)}) collective-permute-start(f32[11,3,3,128]{3,0,2,1:T(8,128)S(1)} %get-tuple-element.54), channel_id=1, source_target_pairs={{17,0},{18,1},{19,2},{20,3},{21,4},{22,5},{23,6},{24,7},{25,8},{26... | collective-permute-start | bytes 152072 | tf_op jit(solution)/shard_map/ppermute | solution.py:28
  197.3 5.6 %collective-permute-start.20 = (f32[11,4,3,128]{3,0,2,1:T(8,128)S(1)}, f32[11,4,3,128]{3,0,2,1:T(8,128)S(1)}, u32[]{:S(2)}, u32[]{:S(2)}) collective-permute-start(f32[11,4,3,128]{3,0,2,1:T(8,128)S(1)} %get-tuple-element.59), channel_id=1, source_target_pairs={{1,0},{2,1},{3,2},{4,3},{5,4},{6,5},{7,6},{8,7},{9,8},{10,9},{11,1... | collective-permute-start | bytes 202760 | tf_op jit(solution)/shard_map/ppermute | solution.py:28
  243.1 3.5 collective-permute-start.25
  248.6 7.3 %collective-permute-start.26 = (f32[11,1,3,128]{3,0,2,1:T(8,128)S(1)}, f32[11,1,3,128]{3,0,2,1:T(8,128)S(1)}, u32[]{:S(2)}, u32[]{:S(2)}) collective-permute-start(f32[11,1,3,128]{3,0,2,1:T(8,128)S(1)} %get-tuple-element.62), channel_id=1, source_target_pairs={{1,32},{2,33},{3,34},{4,35},{5,36},{6,37},{7,38},{8,39},{9,40},{10... | collective-permute-start | bytes 50696 | tf_op jit(solution)/shard_map/ppermute | solution.py:28
  259.8 3.0 collective-permute-start.30
  262.8 4.2 %collective-permute-start.29 = (f32[11,2,3,128]{3,0,2,1:T(8,128)S(1)}, f32[11,2,3,128]{3,0,2,1:T(8,128)S(1)}, u32[]{:S(2)}, u32[]{:S(2)}) collective-permute-start(f32[11,2,3,128]{3,0,2,1:T(8,128)S(1)} %get-tuple-element.67), channel_id=1, source_target_pairs={{1,16},{2,17},{3,18},{4,19},{5,20},{6,21},{7,22},{8,23},{9,24},{10... | collective-permute-start | bytes 101384 | tf_op jit(solution)/shard_map/ppermute | solution.py:28
  269.6 3.4 collective-permute-start.32
  273.1 6.7 %collective-permute-start.34 = (f32[11,2,3,128]{3,0,2,1:T(8,128)S(1)}, f32[11,2,3,128]{3,0,2,1:T(8,128)S(1)}, u32[]{:S(2)}, u32[]{:S(2)}) collective-permute-start(f32[11,2,3,128]{3,0,2,1:T(8,128)S(1)} %get-tuple-element.67), channel_id=1, source_target_pairs={{17,0},{18,1},{19,2},{20,3},{21,4},{22,5},{23,6},{24,7},{25,8},{26... | collective-permute-start | bytes 101384 | tf_op jit(solution)/shard_map/ppermute | solution.py:28
  279.8 3.3 collective-permute-start.33
  289.0 3.8 %collective-permute-done.35 = f32[11,1,3,128]{3,0,2,1:T(8,128)S(1)} collective-permute-done((f32[11,1,3,128]{3,0,2,1:T(8,128)S(1)}, f32[11,1,3,128]{3,0,2,1:T(8,128)S(1)}, u32[]{:S(2)}, u32[]{:S(2)}) %collective-permute-start.35) | collective-permute-done | bytes 16928 | tf_op jit(solution)/shard_map/ppermute | solution.py:28
  314.6 4.7 %collective-permute-start.38 = (f32[5,1,4,128]{3,0,2,1:T(8,128)S(1)}, f32[5,1,4,128]{3,0,2,1:T(8,128)S(1)}, u32[]{:S(2)}, u32[]{:S(2)}) collective-permute-start(f32[5,1,4,128]{3,0,2,1:T(8,128)S(1)} %get-tuple-element.24), channel_id=1, source_target_pairs={{0,16},{16,32},{32,48},{48,64},{64,80},{80,96},{96,112},{1,17},{17... | collective-permute-start | bytes 30728 | tf_op jit(solution)/shard_map/ppermute | solution.py:39
  321.2 3.1 collective-permute-done.39
  326.2 7.0 %collective-permute-start.41 = (f32[5,3,1,128]{3,0,2,1:T(8,128)S(1)}, f32[5,3,1,128]{3,0,2,1:T(8,128)S(1)}, u32[]{:S(2)}, u32[]{:S(2)}) collective-permute-start(f32[5,3,1,128]{3,0,2,1:T(8,128)S(1)} %get-tuple-element.73), channel_id=1, source_target_pairs={{1,0},{2,1},{3,2},{4,3},{5,4},{6,5},{7,6},{8,7},{9,8},{10,9},{11,1... | collective-permute-start | bytes 23048 | tf_op jit(solution)/shard_map/ppermute | solution.py:40
  338.9 2.8 collective-permute-start.42
  343.7 3.1 collective-permute-done.43
  346.8 3.4 collective-permute-start.44
  350.2 4.5 %collective-permute-start.45 = (f32[5,3,1,128]{3,0,2,1:T(8,128)S(1)}, f32[5,3,1,128]{3,0,2,1:T(8,128)S(1)}, u32[]{:S(2)}, u32[]{:S(2)}) collective-permute-start(f32[5,3,1,128]{3,0,2,1:T(8,128)S(1)} %get-tuple-element.71), channel_id=1, source_target_pairs={{1,0},{2,1},{3,2},{4,3},{5,4},{6,5},{7,6},{8,7},{9,8},{10,9},{11,1... | collective-permute-start | bytes 23048 | tf_op jit(solution)/shard_map/ppermute | solution.py:40
  (414 shorter events, 223.1 us)
Async XLA Ops:
  3.2 13.2 %collective-permute-start = (f32[5,1,32,128]{3,0,2,1:T(8,128)S(1)}, f32[5,1,32,128]{3,0,2,1:T(8,128)S(1)}, u32[]{:S(2)}, u32[]{:S(2)}) collective-permute-start(f32[5,1,32,128]{3,0,2,1:T(8,128)S(1)} %get-tuple-element.49), channel_id=1, source_target_pairs={{0,16},{16,32},{32,48},{48,64},{64,80},{80,96},{96,112},{1,17},{17... | collective-permute-start | bytes 245768 | tf_op jit(solution)/shard_map/ppermute | solution.py:39
  7.3 9.1 %collective-permute-start.1 = (f32[5,1,32,128]{3,0,2,1:T(8,128)S(1)}, f32[5,1,32,128]{3,0,2,1:T(8,128)S(1)}, u32[]{:S(2)}, u32[]{:S(2)}) collective-permute-start(f32[5,1,32,128]{3,0,2,1:T(8,128)S(1)} %get-tuple-element.50), channel_id=1, source_target_pairs={{16,0},{32,16},{48,32},{64,48},{80,64},{96,80},{112,96},{17,1},{33... | collective-permute-start | bytes 245768 | tf_op jit(solution)/shard_map/ppermute | solution.py:40
  16.4 9.7 %collective-permute-start.2 = (f32[5,10,1,128]{3,0,2,1:T(8,128)S(1)}, f32[5,10,1,128]{3,0,2,1:T(8,128)S(1)}, u32[]{:S(2)}, u32[]{:S(2)}) collective-permute-start(f32[5,10,1,128]{3,0,2,1:T(8,128)S(1)} %get-tuple-element.41), channel_id=1, source_target_pairs={{0,1},{1,2},{2,3},{3,4},{4,5},{5,6},{6,7},{7,8},{8,9},{9,10},{10,1... | collective-permute-start | bytes 76808 | tf_op jit(solution)/shard_map/ppermute | solution.py:39
  67.1 9.7 %collective-permute-start.6 = (f32[5,10,1,128]{3,0,2,1:T(8,128)S(1)}, f32[5,10,1,128]{3,0,2,1:T(8,128)S(1)}, u32[]{:S(2)}, u32[]{:S(2)}) collective-permute-start(f32[5,10,1,128]{3,0,2,1:T(8,128)S(1)} %get-tuple-element.39), channel_id=1, source_target_pairs={{0,1},{1,2},{2,3},{3,4},{4,5},{5,6},{6,7},{7,8},{8,9},{9,10},{10,1... | collective-permute-start | bytes 76808 | tf_op jit(solution)/shard_map/ppermute | solution.py:39
  69.2 7.6 %collective-permute-start.7 = (f32[5,10,1,128]{3,0,2,1:T(8,128)S(1)}, f32[5,10,1,128]{3,0,2,1:T(8,128)S(1)}, u32[]{:S(2)}, u32[]{:S(2)}) collective-permute-start(f32[5,10,1,128]{3,0,2,1:T(8,128)S(1)} %get-tuple-element.40), channel_id=1, source_target_pairs={{1,0},{2,1},{3,2},{4,3},{5,4},{6,5},{7,6},{8,7},{9,8},{10,9},{11,1... | collective-permute-start | bytes 76808 | tf_op jit(solution)/shard_map/ppermute | solution.py:40
  116.2 9.7 %collective-permute-start.10 = (f32[5,10,1,128]{3,0,2,1:T(8,128)S(1)}, f32[5,10,1,128]{3,0,2,1:T(8,128)S(1)}, u32[]{:S(2)}, u32[]{:S(2)}) collective-permute-start(f32[5,10,1,128]{3,0,2,1:T(8,128)S(1)} %get-tuple-element.37), channel_id=1, source_target_pairs={{0,1},{1,2},{2,3},{3,4},{4,5},{5,6},{6,7},{7,8},{8,9},{9,10},{10,1... | collective-permute-start | bytes 76808 | tf_op jit(solution)/shard_map/ppermute | solution.py:39
  118.6 7.3 %collective-permute-start.11 = (f32[5,10,1,128]{3,0,2,1:T(8,128)S(1)}, f32[5,10,1,128]{3,0,2,1:T(8,128)S(1)}, u32[]{:S(2)}, u32[]{:S(2)}) collective-permute-start(f32[5,10,1,128]{3,0,2,1:T(8,128)S(1)} %get-tuple-element.38), channel_id=1, source_target_pairs={{1,0},{2,1},{3,2},{4,3},{5,4},{6,5},{7,6},{8,7},{9,8},{10,9},{11,1... | collective-permute-start | bytes 76808 | tf_op jit(solution)/shard_map/ppermute | solution.py:40
  164.4 7.9 %collective-permute-start.14 = (f32[5,10,1,128]{3,0,2,1:T(8,128)S(1)}, f32[5,10,1,128]{3,0,2,1:T(8,128)S(1)}, u32[]{:S(2)}, u32[]{:S(2)}) collective-permute-start(f32[5,10,1,128]{3,0,2,1:T(8,128)S(1)} %get-tuple-element.35), channel_id=1, source_target_pairs={{0,1},{1,2},{2,3},{3,4},{4,5},{5,6},{6,7},{7,8},{8,9},{9,10},{10,1... | collective-permute-start | bytes 76808 | tf_op jit(solution)/shard_map/ppermute | solution.py:39
  173.6 31.2 %collective-permute-start.17 = (f32[11,3,16,128]{3,0,2,1:T(8,128)S(1)}, f32[11,3,16,128]{3,0,2,1:T(8,128)S(1)}, u32[]{:S(2)}, u32[]{:S(2)}) collective-permute-start(f32[11,3,16,128]{3,0,2,1:T(8,128)S(1)} %get-tuple-element.56), channel_id=1, source_target_pairs={{0,16},{1,17},{2,18},{3,19},{4,20},{5,21},{6,22},{7,23},{8,24},{9,... | collective-permute-start | bytes 811016 | tf_op jit(solution)/shard_map/ppermute | solution.py:28
  176.5 28.3 %collective-permute-start.22 = (f32[11,3,16,128]{3,0,2,1:T(8,128)S(1)}, f32[11,3,16,128]{3,0,2,1:T(8,128)S(1)}, u32[]{:S(2)}, u32[]{:S(2)}) collective-permute-start(f32[11,3,16,128]{3,0,2,1:T(8,128)S(1)} %get-tuple-element.57), channel_id=1, source_target_pairs={{16,0},{17,1},{18,2},{19,3},{20,4},{21,5},{22,6},{23,7},{24,8},{25... | collective-permute-start | bytes 811016 | tf_op jit(solution)/shard_map/ppermute | solution.py:28
  178.5 11.4 %collective-permute-start.16 = (f32[11,3,3,128]{3,0,2,1:T(8,128)S(1)}, f32[11,3,3,128]{3,0,2,1:T(8,128)S(1)}, u32[]{:S(2)}, u32[]{:S(2)}) collective-permute-start(f32[11,3,3,128]{3,0,2,1:T(8,128)S(1)} %get-tuple-element.52), channel_id=1, source_target_pairs={{0,17},{1,18},{2,19},{3,20},{4,21},{5,22},{6,23},{7,24},{8,25},{9,... | collective-permute-start | bytes 152072 | tf_op jit(solution)/shard_map/ppermute | solution.py:28
  183.0 12.2 %collective-permute-start.18 = (f32[11,3,3,128]{3,0,2,1:T(8,128)S(1)}, f32[11,3,3,128]{3,0,2,1:T(8,128)S(1)}, u32[]{:S(2)}, u32[]{:S(2)}) collective-permute-start(f32[11,3,3,128]{3,0,2,1:T(8,128)S(1)} %get-tuple-element.55), channel_id=1, source_target_pairs={{1,16},{2,17},{3,18},{4,19},{5,20},{6,21},{7,22},{8,23},{9,24},{10... | collective-permute-start | bytes 152072 | tf_op jit(solution)/shard_map/ppermute | solution.py:28
  187.9 9.4 %collective-permute-start.21 = (f32[11,3,3,128]{3,0,2,1:T(8,128)S(1)}, f32[11,3,3,128]{3,0,2,1:T(8,128)S(1)}, u32[]{:S(2)}, u32[]{:S(2)}) collective-permute-start(f32[11,3,3,128]{3,0,2,1:T(8,128)S(1)} %get-tuple-element.53), channel_id=1, source_target_pairs={{16,1},{17,2},{18,3},{19,4},{20,5},{21,6},{22,7},{23,8},{24,9},{25... | collective-permute-start | bytes 152072 | tf_op jit(solution)/shard_map/ppermute | solution.py:28
  189.9 13.0 %collective-permute-start.23 = (f32[11,3,3,128]{3,0,2,1:T(8,128)S(1)}, f32[11,3,3,128]{3,0,2,1:T(8,128)S(1)}, u32[]{:S(2)}, u32[]{:S(2)}) collective-permute-start(f32[11,3,3,128]{3,0,2,1:T(8,128)S(1)} %get-tuple-element.54), channel_id=1, source_target_pairs={{17,0},{18,1},{19,2},{20,3},{21,4},{22,5},{23,6},{24,7},{25,8},{26... | collective-permute-start | bytes 152072 | tf_op jit(solution)/shard_map/ppermute | solution.py:28
  195.2 8.6 %collective-permute-start.19 = (f32[11,4,3,128]{3,0,2,1:T(8,128)S(1)}, f32[11,4,3,128]{3,0,2,1:T(8,128)S(1)}, u32[]{:S(2)}, u32[]{:S(2)}) collective-permute-start(f32[11,4,3,128]{3,0,2,1:T(8,128)S(1)} %get-tuple-element.58), channel_id=1, source_target_pairs={{0,1},{1,2},{2,3},{3,4},{4,5},{5,6},{6,7},{7,8},{8,9},{9,10},{10,1... | collective-permute-start | bytes 202760 | tf_op jit(solution)/shard_map/ppermute | solution.py:28
  197.3 7.5 %collective-permute-start.20 = (f32[11,4,3,128]{3,0,2,1:T(8,128)S(1)}, f32[11,4,3,128]{3,0,2,1:T(8,128)S(1)}, u32[]{:S(2)}, u32[]{:S(2)}) collective-permute-start(f32[11,4,3,128]{3,0,2,1:T(8,128)S(1)} %get-tuple-element.59), channel_id=1, source_target_pairs={{1,0},{2,1},{3,2},{4,3},{5,4},{6,5},{7,6},{8,7},{9,8},{10,9},{11,1... | collective-permute-start | bytes 202760 | tf_op jit(solution)/shard_map/ppermute | solution.py:28
  243.1 23.8 %collective-permute-start.25 = (f32[11,1,8,128]{3,0,2,1:T(8,128)S(1)}, f32[11,1,8,128]{3,0,2,1:T(8,128)S(1)}, u32[]{:S(2)}, u32[]{:S(2)}) collective-permute-start(f32[11,1,8,128]{3,0,2,1:T(8,128)S(1)} %get-tuple-element.65), channel_id=1, source_target_pairs={{0,32},{1,33},{2,34},{3,35},{4,36},{5,37},{6,38},{7,39},{8,40},{9,... | collective-permute-start | bytes 135176 | tf_op jit(solution)/shard_map/ppermute | solution.py:28
  246.7 13.1 %collective-permute-start.24 = (f32[11,1,3,128]{3,0,2,1:T(8,128)S(1)}, f32[11,1,3,128]{3,0,2,1:T(8,128)S(1)}, u32[]{:S(2)}, u32[]{:S(2)}) collective-permute-start(f32[11,1,3,128]{3,0,2,1:T(8,128)S(1)} %get-tuple-element.63), channel_id=1, source_target_pairs={{0,33},{1,34},{2,35},{3,36},{4,37},{5,38},{6,39},{7,40},{8,41},{9,... | collective-permute-start | bytes 50696 | tf_op jit(solution)/shard_map/ppermute | solution.py:28
  248.6 14.2 %collective-permute-start.26 = (f32[11,1,3,128]{3,0,2,1:T(8,128)S(1)}, f32[11,1,3,128]{3,0,2,1:T(8,128)S(1)}, u32[]{:S(2)}, u32[]{:S(2)}) collective-permute-start(f32[11,1,3,128]{3,0,2,1:T(8,128)S(1)} %get-tuple-element.62), channel_id=1, source_target_pairs={{1,32},{2,33},{3,34},{4,35},{5,36},{6,37},{7,38},{8,39},{9,40},{10... | collective-permute-start | bytes 50696 | tf_op jit(solution)/shard_map/ppermute | solution.py:28
  255.9 23.9 %collective-permute-start.28 = (f32[11,2,8,128]{3,0,2,1:T(8,128)S(1)}, f32[11,2,8,128]{3,0,2,1:T(8,128)S(1)}, u32[]{:S(2)}, u32[]{:S(2)}) collective-permute-start(f32[11,2,8,128]{3,0,2,1:T(8,128)S(1)} %pad_maximum_fusion.14), channel_id=1, source_target_pairs={{0,16},{1,17},{2,18},{3,19},{4,20},{5,21},{6,22},{7,23},{8,24},{9,... | collective-permute-start | bytes 270344 | tf_op jit(solution)/shard_map/ppermute | solution.py:28
  257.8 11.8 %collective-permute-start.27 = (f32[11,2,3,128]{3,0,2,1:T(8,128)S(1)}, f32[11,2,3,128]{3,0,2,1:T(8,128)S(1)}, u32[]{:S(2)}, u32[]{:S(2)}) collective-permute-start(f32[11,2,3,128]{3,0,2,1:T(8,128)S(1)} %get-tuple-element.66), channel_id=1, source_target_pairs={{0,17},{1,18},{2,19},{3,20},{4,21},{5,22},{6,23},{7,24},{8,25},{9,... | collective-permute-start | bytes 101384 | tf_op jit(solution)/shard_map/ppermute | solution.py:28
  259.8 23.4 %collective-permute-start.30 = (f32[11,2,3,128]{3,0,2,1:T(8,128)S(1)}, f32[11,2,3,128]{3,0,2,1:T(8,128)S(1)}, u32[]{:S(2)}, u32[]{:S(2)}) collective-permute-start(f32[11,2,3,128]{3,0,2,1:T(8,128)S(1)} %get-tuple-element.66), channel_id=1, source_target_pairs={{0,1},{1,2},{2,3},{3,4},{4,5},{5,6},{6,7},{7,8},{8,9},{9,10},{10,1... | collective-permute-start | bytes 101384 | tf_op jit(solution)/shard_map/ppermute | solution.py:28
  262.8 10.3 %collective-permute-start.29 = (f32[11,2,3,128]{3,0,2,1:T(8,128)S(1)}, f32[11,2,3,128]{3,0,2,1:T(8,128)S(1)}, u32[]{:S(2)}, u32[]{:S(2)}) collective-permute-start(f32[11,2,3,128]{3,0,2,1:T(8,128)S(1)} %get-tuple-element.67), channel_id=1, source_target_pairs={{1,16},{2,17},{3,18},{4,19},{5,20},{6,21},{7,22},{8,23},{9,24},{10... | collective-permute-start | bytes 101384 | tf_op jit(solution)/shard_map/ppermute | solution.py:28
  267.0 18.1 %collective-permute-start.31 = (f32[11,2,3,128]{3,0,2,1:T(8,128)S(1)}, f32[11,2,3,128]{3,0,2,1:T(8,128)S(1)}, u32[]{:S(2)}, u32[]{:S(2)}) collective-permute-start(f32[11,2,3,128]{3,0,2,1:T(8,128)S(1)} %get-tuple-element.67), channel_id=1, source_target_pairs={{1,0},{2,1},{3,2},{4,3},{5,4},{6,5},{7,6},{8,7},{9,8},{10,9},{11,1... | collective-permute-start | bytes 101384 | tf_op jit(solution)/shard_map/ppermute | solution.py:28
  269.6 17.4 %collective-permute-start.32 = (f32[11,2,3,128]{3,0,2,1:T(8,128)S(1)}, f32[11,2,3,128]{3,0,2,1:T(8,128)S(1)}, u32[]{:S(2)}, u32[]{:S(2)}) collective-permute-start(f32[11,2,3,128]{3,0,2,1:T(8,128)S(1)} %get-tuple-element.66), channel_id=1, source_target_pairs={{16,1},{17,2},{18,3},{19,4},{20,5},{21,6},{22,7},{23,8},{24,9},{25... | collective-permute-start | bytes 101384 | tf_op jit(solution)/shard_map/ppermute | solution.py:28
  273.1 15.9 %collective-permute-start.34 = (f32[11,2,3,128]{3,0,2,1:T(8,128)S(1)}, f32[11,2,3,128]{3,0,2,1:T(8,128)S(1)}, u32[]{:S(2)}, u32[]{:S(2)}) collective-permute-start(f32[11,2,3,128]{3,0,2,1:T(8,128)S(1)} %get-tuple-element.67), channel_id=1, source_target_pairs={{17,0},{18,1},{19,2},{20,3},{21,4},{22,5},{23,6},{24,7},{25,8},{26... | collective-permute-start | bytes 101384 | tf_op jit(solution)/shard_map/ppermute | solution.py:28
  279.8 9.2 %collective-permute-start.33 = (f32[11,2,8,128]{3,0,2,1:T(8,128)S(1)}, f32[11,2,8,128]{3,0,2,1:T(8,128)S(1)}, u32[]{:S(2)}, u32[]{:S(2)}) collective-permute-start(f32[11,2,8,128]{3,0,2,1:T(8,128)S(1)} %pad_maximum_fusion.14), channel_id=1, source_target_pairs={{16,0},{17,1},{18,2},{19,3},{20,4},{21,5},{22,6},{23,7},{24,8},{25... | collective-permute-start | bytes 270344 | tf_op jit(solution)/shard_map/ppermute | solution.py:28
  283.1 9.7 %collective-permute-start.36 = (f32[11,1,8,128]{3,0,2,1:T(8,128)S(1)}, f32[11,1,8,128]{3,0,2,1:T(8,128)S(1)}, u32[]{:S(2)}, u32[]{:S(2)}) collective-permute-start(f32[11,1,8,128]{3,0,2,1:T(8,128)S(1)} %get-tuple-element.64), channel_id=1, source_target_pairs={{32,0},{33,1},{34,2},{35,3},{36,4},{37,5},{38,6},{39,7},{40,8},{41... | collective-permute-start | bytes 135176 | tf_op jit(solution)/shard_map/ppermute | solution.py:28
  285.1 7.7 %collective-permute-start.35 = (f32[11,1,3,128]{3,0,2,1:T(8,128)S(1)}, f32[11,1,3,128]{3,0,2,1:T(8,128)S(1)}, u32[]{:S(2)}, u32[]{:S(2)}) collective-permute-start(f32[11,1,3,128]{3,0,2,1:T(8,128)S(1)} %get-tuple-element.60), channel_id=1, source_target_pairs={{32,1},{33,2},{34,3},{35,4},{36,5},{37,6},{38,7},{39,8},{40,9},{41... | collective-permute-start | bytes 50696 | tf_op jit(solution)/shard_map/ppermute | solution.py:28
  324.3 9.0 %collective-permute-start.40 = (f32[5,3,1,128]{3,0,2,1:T(8,128)S(1)}, f32[5,3,1,128]{3,0,2,1:T(8,128)S(1)}, u32[]{:S(2)}, u32[]{:S(2)}) collective-permute-start(f32[5,3,1,128]{3,0,2,1:T(8,128)S(1)} %get-tuple-element.72), channel_id=1, source_target_pairs={{0,1},{1,2},{2,3},{3,4},{4,5},{5,6},{6,7},{7,8},{8,9},{9,10},{10,1... | collective-permute-start | bytes 23048 | tf_op jit(solution)/shard_map/ppermute | solution.py:39
  326.2 7.9 %collective-permute-start.41 = (f32[5,3,1,128]{3,0,2,1:T(8,128)S(1)}, f32[5,3,1,128]{3,0,2,1:T(8,128)S(1)}, u32[]{:S(2)}, u32[]{:S(2)}) collective-permute-start(f32[5,3,1,128]{3,0,2,1:T(8,128)S(1)} %get-tuple-element.73), channel_id=1, source_target_pairs={{1,0},{2,1},{3,2},{4,3},{5,4},{6,5},{7,6},{8,7},{9,8},{10,9},{11,1... | collective-permute-start | bytes 23048 | tf_op jit(solution)/shard_map/ppermute | solution.py:40
  346.8 10.3 %collective-permute-start.44 = (f32[5,3,1,128]{3,0,2,1:T(8,128)S(1)}, f32[5,3,1,128]{3,0,2,1:T(8,128)S(1)}, u32[]{:S(2)}, u32[]{:S(2)}) collective-permute-start(f32[5,3,1,128]{3,0,2,1:T(8,128)S(1)} %get-tuple-element.70), channel_id=1, source_target_pairs={{0,1},{1,2},{2,3},{3,4},{4,5},{5,6},{6,7},{7,8},{8,9},{9,10},{10,1... | collective-permute-start | bytes 23048 | tf_op jit(solution)/shard_map/ppermute | solution.py:39
  (20 other events, 145.0 us)

commit v3 on v0

--- a/solution.py
+++ b/solution.py
@@ -23,16 +23,40 @@
     return block
 
 
+def exchange(block, hx, hy):
+    x_size, y_size = block.shape[1], block.shape[2]
+    nx, ny = lax.axis_size("gx"), lax.axis_size("gy")
+    kx, ky = -(-hx // x_size), -(-hy // y_size)
+    rows = []
+    for dx in range(-kx, kx + 1):
+        xlo, xhi = max(0, -hx - dx * x_size), min(x_size, x_size + hx - dx * x_size)
+        row = []
+        for dy in range(-ky, ky + 1):
+            ylo, yhi = max(0, -hy - dy * y_size), min(y_size, y_size + hy - dy * y_size)
+            piece = block[:, xlo:xhi, ylo:yhi]
+            if dx or dy:
+                pairs = [
+                    ((i + dx) * ny + (j + dy), i * ny + j)
+                    for i in range(nx)
+                    for j in range(ny)
+                    if 0 <= i + dx < nx and 0 <= j + dy < ny
+                ]
+                piece = lax.ppermute(piece, ("gx", "gy"), pairs)
+            row.append(piece)
+        rows.append(jnp.concatenate(row, axis=2))
+    return jnp.concatenate(rows, axis=1)
+
+
 def face_fine(values):
     return with_halo(values, (("gx", 1), ("gy", 2)), 1)
 
 
 def face_coarse(values):
-    return with_halo(values, (("gx", 1), ("gy", 2)), 1)
+    return exchange(values, 1, 1)
 
 
 def face_thin(values):
-    return with_halo(values, (("gx", 1), ("gy", 2)), 1)
+    return exchange(values, 1, 1)
 
 
 def face_residual(values):

time: 359 us -> 447 us (1.25)
  starting transfers between devices: 154 us -> 255 us
  waiting for transfers between devices: 42.5 us -> 25.3 us
    ppermute x0 -> x48, starting transfers between devices: none -> 175 us  [exchange(): piece = lax.ppermute(piece, ('gx', 'gy'), pairs)]
    ppermute x24 -> x12, starting transfers between devices: 82.5 us -> 43.5 us  [with_halo(): lax.ppermute(lax.slice_in_dim(block, 0, width, axis=dim), axis, backward)]
    ppermute x24 -> x12, starting transfers between devices: 71.2 us -> 36.1 us  [with_halo(): lax.ppermute(lax.slice_in_dim(block, block.shape[dim] - width, None, axis...]
    ppermute x24 -> x12, waiting for transfers between devices: 42.4 us -> 20.4 us  [with_halo(): lax.ppermute(lax.slice_in_dim(block, 0, width, axis=dim), axis, backward)]
    ppermute x0 -> x48, waiting for transfers between devices: none -> 4.88 us  [exchange(): piece = lax.ppermute(piece, ('gx', 'gy'), pairs)]
  transfers between devices with their start and end apart: 48 -> 72, of which waited for: 19 -> 17; matrix products, arithmetic and copies ran while one was open for 5% -> 4% of each run, Pallas kernels for 0% -> 0%
where the time goes in v3:
time: 447 us; the launch traced here: 440 us
  starting transfers between devices  255 us (57%)
  matrix products  141 us (32%)
  waiting for transfers between devices  25.3 us (6%)
  local copies, waits for them, and re-layouts  7.66 us (2%)
  other arithmetic  7.6 us (2%)
    ppermute x48, starting transfers between devices, exchange(): piece = lax.ppermute(piece, ('gx', 'gy'), pairs)  175 us
    dot_general x243, matrix products, operate(): jnp.einsum('ab,bxyz->axyz', stencil[offset], shifted, precision=lax.Preci...  141 us
    ppermute x12, starting transfers between devices, with_halo(): lax.ppermute(lax.slice_in_dim(block, 0, width, axis=dim), axis, backward)  43.5 us
    ppermute x12, starting transfers between devices, with_halo(): lax.ppermute(lax.slice_in_dim(block, block.shape[dim] - width, None, axis...  36.1 us
    ppermute x12, waiting for transfers between devices, with_halo(): lax.ppermute(lax.slice_in_dim(block, 0, width, axis=dim), axis, backward)  20.4 us
  transfers between devices with their start and end apart: 72, of which 17 were waited for; matrix products, arithmetic and copies ran while one was open for 4% of the time, Pallas kernels for 0%

profile of v3, /device:TPU:41, one launch (start us, length us, event | category | flops | bytes accessed | tf_op | source)
XLA Modules:
  0.0 439.8 jit_solution(15950321995938515429)
XLA Ops:
  3.1 4.2 collective-permute-start
  20.0 4.4 %collective-permute-start.3 = (f32[5,10,1,128]{3,0,2,1:T(8,128)S(1)}, f32[5,10,1,128]{3,0,2,1:T(8,128)S(1)}, u32[]{:S(2)}, u32[]{:S(2)}) collective-permute-start(f32[5,10,1,128]{3,0,2,1:T(8,128)S(1)} %get-tuple-element.41), channel_id=1, source_target_pairs={{1,0},{2,1},{3,2},{4,3},{5,4},{6,5},{7,6},{8,7},{9,8},{10,9},{11,1... | collective-permute-start | bytes 76808 | tf_op jit(solution)/shard_map/ppermute | solution.py:21
  69.5 5.4 %collective-permute-start.7 = (f32[5,10,1,128]{3,0,2,1:T(8,128)S(1)}, f32[5,10,1,128]{3,0,2,1:T(8,128)S(1)}, u32[]{:S(2)}, u32[]{:S(2)}) collective-permute-start(f32[5,10,1,128]{3,0,2,1:T(8,128)S(1)} %get-tuple-element.39), channel_id=1, source_target_pairs={{1,0},{2,1},{3,2},{4,3},{5,4},{6,5},{7,6},{8,7},{9,8},{10,9},{11,1... | collective-permute-start | bytes 76808 | tf_op jit(solution)/shard_map/ppermute | solution.py:21
  118.9 5.1 %collective-permute-start.11 = (f32[5,10,1,128]{3,0,2,1:T(8,128)S(1)}, f32[5,10,1,128]{3,0,2,1:T(8,128)S(1)}, u32[]{:S(2)}, u32[]{:S(2)}) collective-permute-start(f32[5,10,1,128]{3,0,2,1:T(8,128)S(1)} %get-tuple-element.37), channel_id=1, source_target_pairs={{1,0},{2,1},{3,2},{4,3},{5,4},{6,5},{7,6},{8,7},{9,8},{10,9},{11,1... | collective-permute-start | bytes 76808 | tf_op jit(solution)/shard_map/ppermute | solution.py:21
  160.4 4.3 collective-permute-done.13
  167.2 4.9 %collective-permute-start.15 = (f32[5,10,1,128]{3,0,2,1:T(8,128)S(1)}, f32[5,10,1,128]{3,0,2,1:T(8,128)S(1)}, u32[]{:S(2)}, u32[]{:S(2)}) collective-permute-start(f32[5,10,1,128]{3,0,2,1:T(8,128)S(1)} %get-tuple-element.35), channel_id=1, source_target_pairs={{1,0},{2,1},{3,2},{4,3},{5,4},{6,5},{7,6},{8,7},{9,8},{10,9},{11,1... | collective-permute-start | bytes 76808 | tf_op jit(solution)/shard_map/ppermute | solution.py:21
  180.7 4.8 %collective-permute-start.18 = (f32[5,1,1,128]{3,0,2,1:T(8,128)S(1)}, f32[5,1,1,128]{3,0,2,1:T(8,128)S(1)}, u32[]{:S(2)}, u32[]{:S(2)}) collective-permute-start(f32[5,1,1,128]{3,0,2,1:T(8,128)S(1)} %get-tuple-element.64), channel_id=1, source_target_pairs={{1,16},{2,17},{3,18},{4,19},{5,20},{6,21},{7,22},{8,23},{9,24},{10... | collective-permute-start | bytes 7688 | tf_op jit(solution)/shard_map/ppermute | solution.py:44
  189.4 5.6 %collective-permute-start.23 = (f32[5,1,1,128]{3,0,2,1:T(8,128)S(1)}, f32[5,1,1,128]{3,0,2,1:T(8,128)S(1)}, u32[]{:S(2)}, u32[]{:S(2)}) collective-permute-start(f32[5,1,1,128]{3,0,2,1:T(8,128)S(1)} %get-tuple-element.65), channel_id=1, source_target_pairs={{17,0},{18,1},{19,2},{20,3},{21,4},{22,5},{23,6},{24,7},{25,8},{26... | collective-permute-start | bytes 7688 | tf_op jit(solution)/shard_map/ppermute | solution.py:44
  197.3 5.6 %collective-permute-start.20 = (f32[5,4,1,128]{3,0,2,1:T(8,128)S(1)}, f32[5,4,1,128]{3,0,2,1:T(8,128)S(1)}, u32[]{:S(2)}, u32[]{:S(2)}) collective-permute-start(f32[5,4,1,128]{3,0,2,1:T(8,128)S(1)} %get-tuple-element.63), channel_id=1, source_target_pairs={{1,0},{2,1},{3,2},{4,3},{5,4},{6,5},{7,6},{8,7},{9,8},{10,9},{11,1... | collective-permute-start | bytes 30728 | tf_op jit(solution)/shard_map/ppermute | solution.py:44
  216.7 4.4 collective-permute-start.25
  221.1 6.6 %collective-permute-start.26 = (f32[5,1,1,128]{3,0,2,1:T(8,128)S(1)}, f32[5,1,1,128]{3,0,2,1:T(8,128)S(1)}, u32[]{:S(2)}, u32[]{:S(2)}) collective-permute-start(f32[5,1,1,128]{3,0,2,1:T(8,128)S(1)} %get-tuple-element.56), channel_id=1, source_target_pairs={{1,16},{2,17},{3,18},{4,19},{5,20},{6,21},{7,22},{8,23},{9,24},{10... | collective-permute-start | bytes 7688 | tf_op jit(solution)/shard_map/ppermute | solution.py:44
  231.6 5.6 %collective-permute-start.31 = (f32[5,1,1,128]{3,0,2,1:T(8,128)S(1)}, f32[5,1,1,128]{3,0,2,1:T(8,128)S(1)}, u32[]{:S(2)}, u32[]{:S(2)}) collective-permute-start(f32[5,1,1,128]{3,0,2,1:T(8,128)S(1)} %get-tuple-element.57), channel_id=1, source_target_pairs={{17,0},{18,1},{19,2},{20,3},{21,4},{22,5},{23,6},{24,7},{25,8},{26... | collective-permute-start | bytes 7688 | tf_op jit(solution)/shard_map/ppermute | solution.py:44
  239.6 5.7 %collective-permute-start.28 = (f32[5,4,1,128]{3,0,2,1:T(8,128)S(1)}, f32[5,4,1,128]{3,0,2,1:T(8,128)S(1)}, u32[]{:S(2)}, u32[]{:S(2)}) collective-permute-start(f32[5,4,1,128]{3,0,2,1:T(8,128)S(1)} %get-tuple-element.55), channel_id=1, source_target_pairs={{1,0},{2,1},{3,2},{4,3},{5,4},{6,5},{7,6},{8,7},{9,8},{10,9},{11,1... | collective-permute-start | bytes 30728 | tf_op jit(solution)/shard_map/ppermute | solution.py:44
  256.6 4.4 collective-permute-start.32
  268.6 6.0 %collective-permute-start.35 = (f32[5,6,1,128]{3,0,2,1:T(8,128)S(1)}, f32[5,6,1,128]{3,0,2,1:T(8,128)S(1)}, u32[]{:S(2)}, u32[]{:S(2)}) collective-permute-start(f32[5,6,1,128]{3,0,2,1:T(8,128)S(1)} %get-tuple-element.51), channel_id=1, source_target_pairs={{1,0},{2,1},{3,2},{4,3},{5,4},{6,5},{7,6},{8,7},{9,8},{10,9},{11,1... | collective-permute-start | bytes 46088 | tf_op jit(solution)/shard_map/ppermute | solution.py:21
  282.6 4.6 %collective-permute-start.38 = (f32[5,1,1,128]{3,0,2,1:T(8,128)S(1)}, f32[5,1,1,128]{3,0,2,1:T(8,128)S(1)}, u32[]{:S(2)}, u32[]{:S(2)}) collective-permute-start(f32[5,1,1,128]{3,0,2,1:T(8,128)S(1)} %get-tuple-element.84), channel_id=1, source_target_pairs={{1,16},{2,17},{3,18},{4,19},{5,20},{6,21},{7,22},{8,23},{9,24},{10... | collective-permute-start | bytes 7688 | tf_op jit(solution)/shard_map/ppermute | solution.py:44
  291.1 5.6 %collective-permute-start.43 = (f32[5,1,1,128]{3,0,2,1:T(8,128)S(1)}, f32[5,1,1,128]{3,0,2,1:T(8,128)S(1)}, u32[]{:S(2)}, u32[]{:S(2)}) collective-permute-start(f32[5,1,1,128]{3,0,2,1:T(8,128)S(1)} %get-tuple-element.85), channel_id=1, source_target_pairs={{17,0},{18,1},{19,2},{20,3},{21,4},{22,5},{23,6},{24,7},{25,8},{26... | collective-permute-start | bytes 7688 | tf_op jit(solution)/shard_map/ppermute | solution.py:44
  299.1 5.7 %collective-permute-start.40 = (f32[5,2,1,128]{3,0,2,1:T(8,128)S(1)}, f32[5,2,1,128]{3,0,2,1:T(8,128)S(1)}, u32[]{:S(2)}, u32[]{:S(2)}) collective-permute-start(f32[5,2,1,128]{3,0,2,1:T(8,128)S(1)} %get-tuple-element.83), channel_id=1, source_target_pairs={{1,0},{2,1},{3,2},{4,3},{5,4},{6,5},{7,6},{8,7},{9,8},{10,9},{11,1... | collective-permute-start | bytes 15368 | tf_op jit(solution)/shard_map/ppermute | solution.py:44
  313.5 4.4 collective-permute-start.45
  317.9 6.6 %collective-permute-start.46 = (f32[5,1,1,128]{3,0,2,1:T(8,128)S(1)}, f32[5,1,1,128]{3,0,2,1:T(8,128)S(1)}, u32[]{:S(2)}, u32[]{:S(2)}) collective-permute-start(f32[5,1,1,128]{3,0,2,1:T(8,128)S(1)} %get-tuple-element.76), channel_id=1, source_target_pairs={{1,16},{2,17},{3,18},{4,19},{5,20},{6,21},{7,22},{8,23},{9,24},{10... | collective-permute-start | bytes 7688 | tf_op jit(solution)/shard_map/ppermute | solution.py:44
  328.4 5.6 %collective-permute-start.51 = (f32[5,1,1,128]{3,0,2,1:T(8,128)S(1)}, f32[5,1,1,128]{3,0,2,1:T(8,128)S(1)}, u32[]{:S(2)}, u32[]{:S(2)}) collective-permute-start(f32[5,1,1,128]{3,0,2,1:T(8,128)S(1)} %get-tuple-element.77), channel_id=1, source_target_pairs={{17,0},{18,1},{19,2},{20,3},{21,4},{22,5},{23,6},{24,7},{25,8},{26... | collective-permute-start | bytes 7688 | tf_op jit(solution)/shard_map/ppermute | solution.py:44
  336.4 5.5 %collective-permute-start.48 = (f32[5,2,1,128]{3,0,2,1:T(8,128)S(1)}, f32[5,2,1,128]{3,0,2,1:T(8,128)S(1)}, u32[]{:S(2)}, u32[]{:S(2)}) collective-permute-start(f32[5,2,1,128]{3,0,2,1:T(8,128)S(1)} %get-tuple-element.75), channel_id=1, source_target_pairs={{1,0},{2,1},{3,2},{4,3},{5,4},{6,5},{7,6},{8,7},{9,8},{10,9},{11,1... | collective-permute-start | bytes 15368 | tf_op jit(solution)/shard_map/ppermute | solution.py:44
  348.7 4.5 %collective-permute-start.52 = (f32[5,1,8,128]{3,0,2,1:T(8,128)S(1)}, f32[5,1,8,128]{3,0,2,1:T(8,128)S(1)}, u32[]{:S(2)}, u32[]{:S(2)}) collective-permute-start(f32[5,1,8,128]{3,0,2,1:T(8,128)S(1)} %get-tuple-element.72), channel_id=1, source_target_pairs={{0,16},{16,32},{32,48},{48,64},{64,80},{80,96},{96,112},{1,17},{17... | collective-permute-start | bytes 61448 | tf_op jit(solution)/shard_map/ppermute | solution.py:18
  360.3 6.0 %collective-permute-start.55 = (f32[5,4,1,128]{3,0,2,1:T(8,128)S(1)}, f32[5,4,1,128]{3,0,2,1:T(8,128)S(1)}, u32[]{:S(2)}, u32[]{:S(2)}) collective-permute-start(f32[5,4,1,128]{3,0,2,1:T(8,128)S(1)} %get-tuple-element.71), channel_id=1, source_target_pairs={{1,0},{2,1},{3,2},{4,3},{5,4},{6,5},{7,6},{8,7},{9,8},{10,9},{11,1... | collective-permute-start | bytes 30728 | tf_op jit(solution)/shard_map/ppermute | solution.py:21
  372.0 4.9 %collective-permute-start.56 = (f32[5,1,1,128]{3,0,2,1:T(8,128)S(1)}, f32[5,1,1,128]{3,0,2,1:T(8,128)S(1)}, u32[]{:S(2)}, u32[]{:S(2)}) collective-permute-start(f32[5,1,1,128]{3,0,2,1:T(8,128)S(1)} %get-tuple-element.121), channel_id=1, source_target_pairs={{0,17},{1,18},{2,19},{3,20},{4,21},{5,22},{6,23},{7,24},{8,25},{9,... | collective-permute-start | bytes 7688 | tf_op jit(solution)/shard_map/ppermute | solution.py:44
  376.9 4.5 %collective-permute-start.58 = (f32[5,1,1,128]{3,0,2,1:T(8,128)S(1)}, f32[5,1,1,128]{3,0,2,1:T(8,128)S(1)}, u32[]{:S(2)}, u32[]{:S(2)}) collective-permute-start(f32[5,1,1,128]{3,0,2,1:T(8,128)S(1)} %get-tuple-element.122), channel_id=1, source_target_pairs={{1,16},{2,17},{3,18},{4,19},{5,20},{6,21},{7,22},{8,23},{9,24},{10... | collective-permute-start | bytes 7688 | tf_op jit(solution)/shard_map/ppermute | solution.py:44
  383.4 5.5 %collective-permute-start.60 = (f32[5,1,1,128]{3,0,2,1:T(8,128)S(1)}, f32[5,1,1,128]{3,0,2,1:T(8,128)S(1)}, u32[]{:S(2)}, u32[]{:S(2)}) collective-permute-start(f32[5,1,1,128]{3,0,2,1:T(8,128)S(1)} %get-tuple-element.122), channel_id=1, source_target_pairs={{1,0},{2,1},{3,2},{4,3},{5,4},{6,5},{7,6},{8,7},{9,8},{10,9},{11,1... | collective-permute-start | bytes 7688 | tf_op jit(solution)/shard_map/ppermute | solution.py:44
  390.9 5.1 %collective-permute-start.63 = (f32[5,1,1,128]{3,0,2,1:T(8,128)S(1)}, f32[5,1,1,128]{3,0,2,1:T(8,128)S(1)}, u32[]{:S(2)}, u32[]{:S(2)}) collective-permute-start(f32[5,1,1,128]{3,0,2,1:T(8,128)S(1)} %get-tuple-element.122), channel_id=1, source_target_pairs={{17,0},{18,1},{19,2},{20,3},{21,4},{22,5},{23,6},{24,7},{25,8},{26... | collective-permute-start | bytes 7688 | tf_op jit(solution)/shard_map/ppermute | solution.py:44
  401.7 4.4 %collective-permute-start.65 = (f32[5,1,4,128]{3,0,2,1:T(8,128)S(1)}, f32[5,1,4,128]{3,0,2,1:T(8,128)S(1)}, u32[]{:S(2)}, u32[]{:S(2)}) collective-permute-start(f32[5,1,4,128]{3,0,2,1:T(8,128)S(1)} %fusion.245), channel_id=1, source_target_pairs={{0,16},{1,17},{2,18},{3,19},{4,20},{5,21},{6,22},{7,23},{8,24},{9,... | collective-permute-start | bytes 30728 | tf_op jit(solution)/shard_map/ppermute | solution.py:44
  410.0 6.9 %collective-permute-start.66 = (f32[5,1,1,128]{3,0,2,1:T(8,128)S(1)}, f32[5,1,1,128]{3,0,2,1:T(8,128)S(1)}, u32[]{:S(2)}, u32[]{:S(2)}) collective-permute-start(f32[5,1,1,128]{3,0,2,1:T(8,128)S(1)} %get-tuple-element.120), channel_id=1, source_target_pairs={{1,16},{2,17},{3,18},{4,19},{5,20},{6,21},{7,22},{8,23},{9,24},{10... | collective-permute-start | bytes 7688 | tf_op jit(solution)/shard_map/ppermute | solution.py:44
  418.9 5.5 %collective-permute-start.68 = (f32[5,1,1,128]{3,0,2,1:T(8,128)S(1)}, f32[5,1,1,128]{3,0,2,1:T(8,128)S(1)}, u32[]{:S(2)}, u32[]{:S(2)}) collective-permute-start(f32[5,1,1,128]{3,0,2,1:T(8,128)S(1)} %get-tuple-element.120), channel_id=1, source_target_pairs={{1,0},{2,1},{3,2},{4,3},{5,4},{6,5},{7,6},{8,7},{9,8},{10,9},{11,1... | collective-permute-start | bytes 7688 | tf_op jit(solution)/shard_map/ppermute | solution.py:44
  426.3 5.5 %collective-permute-start.71 = (f32[5,1,1,128]{3,0,2,1:T(8,128)S(1)}, f32[5,1,1,128]{3,0,2,1:T(8,128)S(1)}, u32[]{:S(2)}, u32[]{:S(2)}) collective-permute-start(f32[5,1,1,128]{3,0,2,1:T(8,128)S(1)} %get-tuple-element.120), channel_id=1, source_target_pairs={{17,0},{18,1},{19,2},{20,3},{21,4},{22,5},{23,6},{24,7},{25,8},{26... | collective-permute-start | bytes 7688 | tf_op jit(solution)/shard_map/ppermute | solution.py:44
  (484 shorter events, 268.0 us)
Async XLA Ops:
  3.1 13.7 %collective-permute-start = (f32[5,1,32,128]{3,0,2,1:T(8,128)S(1)}, f32[5,1,32,128]{3,0,2,1:T(8,128)S(1)}, u32[]{:S(2)}, u32[]{:S(2)}) collective-permute-start(f32[5,1,32,128]{3,0,2,1:T(8,128)S(1)} %get-tuple-element.48), channel_id=1, source_target_pairs={{0,16},{16,32},{32,48},{48,64},{64,80},{80,96},{96,112},{1,17},{17... | collective-permute-start | bytes 245768 | tf_op jit(solution)/shard_map/ppermute | solution.py:18
  174.0 15.4 %collective-permute-start.16 = (f32[5,1,1,128]{3,0,2,1:T(8,128)S(1)}, f32[5,1,1,128]{3,0,2,1:T(8,128)S(1)}, u32[]{:S(2)}, u32[]{:S(2)}) collective-permute-start(f32[5,1,1,128]{3,0,2,1:T(8,128)S(1)} %get-tuple-element.67), channel_id=1, source_target_pairs={{0,17},{1,18},{2,19},{3,20},{4,21},{5,22},{6,23},{7,24},{8,25},{9,... | collective-permute-start | bytes 7688 | tf_op jit(solution)/shard_map/ppermute | solution.py:44
  177.9 19.5 %collective-permute-start.17 = (f32[5,1,16,128]{3,0,2,1:T(8,128)S(1)}, f32[5,1,16,128]{3,0,2,1:T(8,128)S(1)}, u32[]{:S(2)}, u32[]{:S(2)}) collective-permute-start(f32[5,1,16,128]{3,0,2,1:T(8,128)S(1)} %get-tuple-element.68), channel_id=1, source_target_pairs={{0,16},{1,17},{2,18},{3,19},{4,20},{5,21},{6,22},{7,23},{8,24},{9,... | collective-permute-start | bytes 122888 | tf_op jit(solution)/shard_map/ppermute | solution.py:44
  180.7 22.4 %collective-permute-start.18 = (f32[5,1,1,128]{3,0,2,1:T(8,128)S(1)}, f32[5,1,1,128]{3,0,2,1:T(8,128)S(1)}, u32[]{:S(2)}, u32[]{:S(2)}) collective-permute-start(f32[5,1,1,128]{3,0,2,1:T(8,128)S(1)} %get-tuple-element.64), channel_id=1, source_target_pairs={{1,16},{2,17},{3,18},{4,19},{5,20},{6,21},{7,22},{8,23},{9,24},{10... | collective-permute-start | bytes 7688 | tf_op jit(solution)/shard_map/ppermute | solution.py:44
  185.5 17.5 %collective-permute-start.22 = (f32[5,1,16,128]{3,0,2,1:T(8,128)S(1)}, f32[5,1,16,128]{3,0,2,1:T(8,128)S(1)}, u32[]{:S(2)}, u32[]{:S(2)}) collective-permute-start(f32[5,1,16,128]{3,0,2,1:T(8,128)S(1)} %get-tuple-element.69), channel_id=1, source_target_pairs={{16,0},{17,1},{18,2},{19,3},{20,4},{21,5},{22,6},{23,7},{24,8},{25... | collective-permute-start | bytes 122888 | tf_op jit(solution)/shard_map/ppermute | solution.py:44
  189.4 13.7 %collective-permute-start.23 = (f32[5,1,1,128]{3,0,2,1:T(8,128)S(1)}, f32[5,1,1,128]{3,0,2,1:T(8,128)S(1)}, u32[]{:S(2)}, u32[]{:S(2)}) collective-permute-start(f32[5,1,1,128]{3,0,2,1:T(8,128)S(1)} %get-tuple-element.65), channel_id=1, source_target_pairs={{17,0},{18,1},{19,2},{20,3},{21,4},{22,5},{23,6},{24,7},{25,8},{26... | collective-permute-start | bytes 7688 | tf_op jit(solution)/shard_map/ppermute | solution.py:44
  214.8 16.8 %collective-permute-start.24 = (f32[5,1,1,128]{3,0,2,1:T(8,128)S(1)}, f32[5,1,1,128]{3,0,2,1:T(8,128)S(1)}, u32[]{:S(2)}, u32[]{:S(2)}) collective-permute-start(f32[5,1,1,128]{3,0,2,1:T(8,128)S(1)} %get-tuple-element.59), channel_id=1, source_target_pairs={{0,17},{1,18},{2,19},{3,20},{4,21},{5,22},{6,23},{7,24},{8,25},{9,... | collective-permute-start | bytes 7688 | tf_op jit(solution)/shard_map/ppermute | solution.py:44
  216.7 22.9 %collective-permute-start.25 = (f32[5,1,16,128]{3,0,2,1:T(8,128)S(1)}, f32[5,1,16,128]{3,0,2,1:T(8,128)S(1)}, u32[]{:S(2)}, u32[]{:S(2)}) collective-permute-start(f32[5,1,16,128]{3,0,2,1:T(8,128)S(1)} %get-tuple-element.60), channel_id=1, source_target_pairs={{0,16},{1,17},{2,18},{3,19},{4,20},{5,21},{6,22},{7,23},{8,24},{9,... | collective-permute-start | bytes 122888 | tf_op jit(solution)/shard_map/ppermute | solution.py:44
  221.1 24.2 %collective-permute-start.26 = (f32[5,1,1,128]{3,0,2,1:T(8,128)S(1)}, f32[5,1,1,128]{3,0,2,1:T(8,128)S(1)}, u32[]{:S(2)}, u32[]{:S(2)}) collective-permute-start(f32[5,1,1,128]{3,0,2,1:T(8,128)S(1)} %get-tuple-element.56), channel_id=1, source_target_pairs={{1,16},{2,17},{3,18},{4,19},{5,20},{6,21},{7,22},{8,23},{9,24},{10... | collective-permute-start | bytes 7688 | tf_op jit(solution)/shard_map/ppermute | solution.py:44
  227.7 17.5 %collective-permute-start.30 = (f32[5,1,16,128]{3,0,2,1:T(8,128)S(1)}, f32[5,1,16,128]{3,0,2,1:T(8,128)S(1)}, u32[]{:S(2)}, u32[]{:S(2)}) collective-permute-start(f32[5,1,16,128]{3,0,2,1:T(8,128)S(1)} %get-tuple-element.61), channel_id=1, source_target_pairs={{16,0},{17,1},{18,2},{19,3},{20,4},{21,5},{22,6},{23,7},{24,8},{25... | collective-permute-start | bytes 122888 | tf_op jit(solution)/shard_map/ppermute | solution.py:44
  231.6 13.7 %collective-permute-start.31 = (f32[5,1,1,128]{3,0,2,1:T(8,128)S(1)}, f32[5,1,1,128]{3,0,2,1:T(8,128)S(1)}, u32[]{:S(2)}, u32[]{:S(2)}) collective-permute-start(f32[5,1,1,128]{3,0,2,1:T(8,128)S(1)} %get-tuple-element.57), channel_id=1, source_target_pairs={{17,0},{18,1},{19,2},{20,3},{21,4},{22,5},{23,6},{24,7},{25,8},{26... | collective-permute-start | bytes 7688 | tf_op jit(solution)/shard_map/ppermute | solution.py:44
  275.9 15.2 %collective-permute-start.36 = (f32[5,1,1,128]{3,0,2,1:T(8,128)S(1)}, f32[5,1,1,128]{3,0,2,1:T(8,128)S(1)}, u32[]{:S(2)}, u32[]{:S(2)}) collective-permute-start(f32[5,1,1,128]{3,0,2,1:T(8,128)S(1)} %get-tuple-element.87), channel_id=1, source_target_pairs={{0,17},{1,18},{2,19},{3,20},{4,21},{5,22},{6,23},{7,24},{8,25},{9,... | collective-permute-start | bytes 7688 | tf_op jit(solution)/shard_map/ppermute | solution.py:44
  279.9 19.2 %collective-permute-start.37 = (f32[5,1,8,128]{3,0,2,1:T(8,128)S(1)}, f32[5,1,8,128]{3,0,2,1:T(8,128)S(1)}, u32[]{:S(2)}, u32[]{:S(2)}) collective-permute-start(f32[5,1,8,128]{3,0,2,1:T(8,128)S(1)} %get-tuple-element.88), channel_id=1, source_target_pairs={{0,16},{1,17},{2,18},{3,19},{4,20},{5,21},{6,22},{7,23},{8,24},{9,... | collective-permute-start | bytes 61448 | tf_op jit(solution)/shard_map/ppermute | solution.py:44
  282.6 22.2 %collective-permute-start.38 = (f32[5,1,1,128]{3,0,2,1:T(8,128)S(1)}, f32[5,1,1,128]{3,0,2,1:T(8,128)S(1)}, u32[]{:S(2)}, u32[]{:S(2)}) collective-permute-start(f32[5,1,1,128]{3,0,2,1:T(8,128)S(1)} %get-tuple-element.84), channel_id=1, source_target_pairs={{1,16},{2,17},{3,18},{4,19},{5,20},{6,21},{7,22},{8,23},{9,24},{10... | collective-permute-start | bytes 7688 | tf_op jit(solution)/shard_map/ppermute | solution.py:44
  287.2 17.6 %collective-permute-start.42 = (f32[5,1,8,128]{3,0,2,1:T(8,128)S(1)}, f32[5,1,8,128]{3,0,2,1:T(8,128)S(1)}, u32[]{:S(2)}, u32[]{:S(2)}) collective-permute-start(f32[5,1,8,128]{3,0,2,1:T(8,128)S(1)} %get-tuple-element.89), channel_id=1, source_target_pairs={{16,0},{17,1},{18,2},{19,3},{20,4},{21,5},{22,6},{23,7},{24,8},{25... | collective-permute-start | bytes 61448 | tf_op jit(solution)/shard_map/ppermute | solution.py:44
  291.1 13.7 %collective-permute-start.43 = (f32[5,1,1,128]{3,0,2,1:T(8,128)S(1)}, f32[5,1,1,128]{3,0,2,1:T(8,128)S(1)}, u32[]{:S(2)}, u32[]{:S(2)}) collective-permute-start(f32[5,1,1,128]{3,0,2,1:T(8,128)S(1)} %get-tuple-element.85), channel_id=1, source_target_pairs={{17,0},{18,1},{19,2},{20,3},{21,4},{22,5},{23,6},{24,7},{25,8},{26... | collective-permute-start | bytes 7688 | tf_op jit(solution)/shard_map/ppermute | solution.py:44
  311.6 16.8 %collective-permute-start.44 = (f32[5,1,1,128]{3,0,2,1:T(8,128)S(1)}, f32[5,1,1,128]{3,0,2,1:T(8,128)S(1)}, u32[]{:S(2)}, u32[]{:S(2)}) collective-permute-start(f32[5,1,1,128]{3,0,2,1:T(8,128)S(1)} %get-tuple-element.79), channel_id=1, source_target_pairs={{0,17},{1,18},{2,19},{3,20},{4,21},{5,22},{6,23},{7,24},{8,25},{9,... | collective-permute-start | bytes 7688 | tf_op jit(solution)/shard_map/ppermute | solution.py:44
  313.5 22.9 %collective-permute-start.45 = (f32[5,1,8,128]{3,0,2,1:T(8,128)S(1)}, f32[5,1,8,128]{3,0,2,1:T(8,128)S(1)}, u32[]{:S(2)}, u32[]{:S(2)}) collective-permute-start(f32[5,1,8,128]{3,0,2,1:T(8,128)S(1)} %get-tuple-element.80), channel_id=1, source_target_pairs={{0,16},{1,17},{2,18},{3,19},{4,20},{5,21},{6,22},{7,23},{8,24},{9,... | collective-permute-start | bytes 61448 | tf_op jit(solution)/shard_map/ppermute | solution.py:44
  317.9 24.0 %collective-permute-start.46 = (f32[5,1,1,128]{3,0,2,1:T(8,128)S(1)}, f32[5,1,1,128]{3,0,2,1:T(8,128)S(1)}, u32[]{:S(2)}, u32[]{:S(2)}) collective-permute-start(f32[5,1,1,128]{3,0,2,1:T(8,128)S(1)} %get-tuple-element.76), channel_id=1, source_target_pairs={{1,16},{2,17},{3,18},{4,19},{5,20},{6,21},{7,22},{8,23},{9,24},{10... | collective-permute-start | bytes 7688 | tf_op jit(solution)/shard_map/ppermute | solution.py:44
  324.6 17.3 %collective-permute-start.50 = (f32[5,1,8,128]{3,0,2,1:T(8,128)S(1)}, f32[5,1,8,128]{3,0,2,1:T(8,128)S(1)}, u32[]{:S(2)}, u32[]{:S(2)}) collective-permute-start(f32[5,1,8,128]{3,0,2,1:T(8,128)S(1)} %get-tuple-element.81), channel_id=1, source_target_pairs={{16,0},{17,1},{18,2},{19,3},{20,4},{21,5},{22,6},{23,7},{24,8},{25... | collective-permute-start | bytes 61448 | tf_op jit(solution)/shard_map/ppermute | solution.py:44
  328.4 13.5 %collective-permute-start.51 = (f32[5,1,1,128]{3,0,2,1:T(8,128)S(1)}, f32[5,1,1,128]{3,0,2,1:T(8,128)S(1)}, u32[]{:S(2)}, u32[]{:S(2)}) collective-permute-start(f32[5,1,1,128]{3,0,2,1:T(8,128)S(1)} %get-tuple-element.77), channel_id=1, source_target_pairs={{17,0},{18,1},{19,2},{20,3},{21,4},{22,5},{23,6},{24,7},{25,8},{26... | collective-permute-start | bytes 7688 | tf_op jit(solution)/shard_map/ppermute | solution.py:44
  367.3 29.5 %collective-permute-start.57 = (f32[5,1,4,128]{3,0,2,1:T(8,128)S(1)}, f32[5,1,4,128]{3,0,2,1:T(8,128)S(1)}, u32[]{:S(2)}, u32[]{:S(2)}) collective-permute-start(f32[5,1,4,128]{3,0,2,1:T(8,128)S(1)} %get-tuple-element.28), channel_id=1, source_target_pairs={{0,16},{1,17},{2,18},{3,19},{4,20},{5,21},{6,22},{7,23},{8,24},{9,... | collective-permute-start | bytes 30728 | tf_op jit(solution)/shard_map/ppermute | solution.py:44
  370.1 26.8 %collective-permute-start.62 = (f32[5,1,4,128]{3,0,2,1:T(8,128)S(1)}, f32[5,1,4,128]{3,0,2,1:T(8,128)S(1)}, u32[]{:S(2)}, u32[]{:S(2)}) collective-permute-start(f32[5,1,4,128]{3,0,2,1:T(8,128)S(1)} %get-tuple-element.28), channel_id=1, source_target_pairs={{16,0},{17,1},{18,2},{19,3},{20,4},{21,5},{22,6},{23,7},{24,8},{25... | collective-permute-start | bytes 30728 | tf_op jit(solution)/shard_map/ppermute | solution.py:44
  372.0 11.4 %collective-permute-start.56 = (f32[5,1,1,128]{3,0,2,1:T(8,128)S(1)}, f32[5,1,1,128]{3,0,2,1:T(8,128)S(1)}, u32[]{:S(2)}, u32[]{:S(2)}) collective-permute-start(f32[5,1,1,128]{3,0,2,1:T(8,128)S(1)} %get-tuple-element.121), channel_id=1, source_target_pairs={{0,17},{1,18},{2,19},{3,20},{4,21},{5,22},{6,23},{7,24},{8,25},{9,... | collective-permute-start | bytes 7688 | tf_op jit(solution)/shard_map/ppermute | solution.py:44
  376.9 12.0 %collective-permute-start.58 = (f32[5,1,1,128]{3,0,2,1:T(8,128)S(1)}, f32[5,1,1,128]{3,0,2,1:T(8,128)S(1)}, u32[]{:S(2)}, u32[]{:S(2)}) collective-permute-start(f32[5,1,1,128]{3,0,2,1:T(8,128)S(1)} %get-tuple-element.122), channel_id=1, source_target_pairs={{1,16},{2,17},{3,18},{4,19},{5,20},{6,21},{7,22},{8,23},{9,24},{10... | collective-permute-start | bytes 7688 | tf_op jit(solution)/shard_map/ppermute | solution.py:44
  383.4 12.5 %collective-permute-start.60 = (f32[5,1,1,128]{3,0,2,1:T(8,128)S(1)}, f32[5,1,1,128]{3,0,2,1:T(8,128)S(1)}, u32[]{:S(2)}, u32[]{:S(2)}) collective-permute-start(f32[5,1,1,128]{3,0,2,1:T(8,128)S(1)} %get-tuple-element.122), channel_id=1, source_target_pairs={{1,0},{2,1},{3,2},{4,3},{5,4},{6,5},{7,6},{8,7},{9,8},{10,9},{11,1... | collective-permute-start | bytes 7688 | tf_op jit(solution)/shard_map/ppermute | solution.py:44
  401.7 32.4 %collective-permute-start.65 = (f32[5,1,4,128]{3,0,2,1:T(8,128)S(1)}, f32[5,1,4,128]{3,0,2,1:T(8,128)S(1)}, u32[]{:S(2)}, u32[]{:S(2)}) collective-permute-start(f32[5,1,4,128]{3,0,2,1:T(8,128)S(1)} %fusion.245), channel_id=1, source_target_pairs={{0,16},{1,17},{2,18},{3,19},{4,20},{5,21},{6,22},{7,23},{8,24},{9,... | collective-permute-start | bytes 30728 | tf_op jit(solution)/shard_map/ppermute | solution.py:44
  406.1 28.0 %collective-permute-start.70 = (f32[5,1,4,128]{3,0,2,1:T(8,128)S(1)}, f32[5,1,4,128]{3,0,2,1:T(8,128)S(1)}, u32[]{:S(2)}, u32[]{:S(2)}) collective-permute-start(f32[5,1,4,128]{3,0,2,1:T(8,128)S(1)} %fusion.245), channel_id=1, source_target_pairs={{16,0},{17,1},{18,2},{19,3},{20,4},{21,5},{22,6},{23,7},{24,8},{25... | collective-permute-start | bytes 30728 | tf_op jit(solution)/shard_map/ppermute | solution.py:44
  408.1 10.8 %collective-permute-start.64 = (f32[5,1,1,128]{3,0,2,1:T(8,128)S(1)}, f32[5,1,1,128]{3,0,2,1:T(8,128)S(1)}, u32[]{:S(2)}, u32[]{:S(2)}) collective-permute-start(f32[5,1,1,128]{3,0,2,1:T(8,128)S(1)} %get-tuple-element.119), channel_id=1, source_target_pairs={{0,17},{1,18},{2,19},{3,20},{4,21},{5,22},{6,23},{7,24},{8,25},{9,... | collective-permute-start | bytes 7688 | tf_op jit(solution)/shard_map/ppermute | solution.py:44
  410.0 14.4 %collective-permute-start.66 = (f32[5,1,1,128]{3,0,2,1:T(8,128)S(1)}, f32[5,1,1,128]{3,0,2,1:T(8,128)S(1)}, u32[]{:S(2)}, u32[]{:S(2)}) collective-permute-start(f32[5,1,1,128]{3,0,2,1:T(8,128)S(1)} %get-tuple-element.120), channel_id=1, source_target_pairs={{1,16},{2,17},{3,18},{4,19},{5,20},{6,21},{7,22},{8,23},{9,24},{10... | collective-permute-start | bytes 7688 | tf_op jit(solution)/shard_map/ppermute | solution.py:44
  418.9 15.2 %collective-permute-start.68 = (f32[5,1,1,128]{3,0,2,1:T(8,128)S(1)}, f32[5,1,1,128]{3,0,2,1:T(8,128)S(1)}, u32[]{:S(2)}, u32[]{:S(2)}) collective-permute-start(f32[5,1,1,128]{3,0,2,1:T(8,128)S(1)} %get-tuple-element.120), channel_id=1, source_target_pairs={{1,0},{2,1},{3,2},{4,3},{5,4},{6,5},{7,6},{8,7},{9,8},{10,9},{11,1... | collective-permute-start | bytes 7688 | tf_op jit(solution)/shard_map/ppermute | solution.py:44
  424.4 9.7 %collective-permute-start.69 = (f32[5,1,1,128]{3,0,2,1:T(8,128)S(1)}, f32[5,1,1,128]{3,0,2,1:T(8,128)S(1)}, u32[]{:S(2)}, u32[]{:S(2)}) collective-permute-start(f32[5,1,1,128]{3,0,2,1:T(8,128)S(1)} %get-tuple-element.119), channel_id=1, source_target_pairs={{16,1},{17,2},{18,3},{19,4},{20,5},{21,6},{22,7},{23,8},{24,9},{25... | collective-permute-start | bytes 7688 | tf_op jit(solution)/shard_map/ppermute | solution.py:44
  (46 other events, 397.7 us)

commit v4 on v0

--- a/solution.py
+++ b/solution.py
@@ -53,7 +53,7 @@
             shift_z : shift_z + extent_z,
         ]
         summed = summed + jnp.einsum(
-            "ab,bxyz->axyz", stencil[offset], shifted, precision=lax.Precision.HIGHEST
+            "ab,bxyz->axyz", stencil[offset], shifted, precision=lax.Precision.HIGH
         )
     return conduct * rock_share[None] * summed
 

time: 359 us -> 317 us (0.88)
  matrix products: 140 us -> 95 us
    dot_general x243, matrix products: 140 us -> 95 us  [operate(): jnp.einsum('ab,bxyz->axyz', stencil[offset], shifted, precision=lax.Preci...]
    ppermute x24, starting transfers between devices: 71.2 us -> 75.3 us  [with_halo(): lax.ppermute(lax.slice_in_dim(block, block.shape[dim] - width, None, axis...]
    ppermute x24, starting transfers between devices: 82.5 us -> 78.9 us  [with_halo(): lax.ppermute(lax.slice_in_dim(block, 0, width, axis=dim), axis, backward)]
where the time goes in v4:
time: 317 us; the launch traced here: 313 us
  starting transfers between devices  154 us (49%)
  matrix products  95 us (30%)
  waiting for transfers between devices  44.3 us (14%)
  local copies, waits for them, and re-layouts  8.85 us (3%)
  other arithmetic  7.62 us (2%)
  between operations  3.26 us (1%)
    dot_general x243, matrix products, operate(): jnp.einsum('ab,bxyz->axyz', stencil[offset], shifted, precision=lax.Preci...  95 us
    ppermute x24, starting transfers between devices, with_halo(): lax.ppermute(lax.slice_in_dim(block, 0, width, axis=dim), axis, backward)  78.9 us
    ppermute x24, starting transfers between devices, with_halo(): lax.ppermute(lax.slice_in_dim(block, block.shape[dim] - width, None, axis...  75.3 us
    ppermute x24, waiting for transfers between devices, with_halo(): lax.ppermute(lax.slice_in_dim(block, 0, width, axis=dim), axis, backward)  44.3 us
    unnamed x43, local copies, waits for them, and re-layouts  7.8 us
  transfers between devices with their start and end apart: 48, of which 19 were waited for; matrix products, arithmetic and copies ran while one was open for 5% of the time, Pallas kernels for 0%

profile of v4, /device:TPU:41, one launch (start us, length us, event | category | flops | bytes accessed | tf_op | source)
XLA Modules:
  0.0 313.2 jit_solution(600536044369310976)
XLA Ops:
  3.1 4.2 %collective-permute-start = (f32[5,1,32,128]{3,0,2,1:T(8,128)S(1)}, f32[5,1,32,128]{3,0,2,1:T(8,128)S(1)}, u32[]{:S(2)}, u32[]{:S(2)}) collective-permute-start(f32[5,1,32,128]{3,0,2,1:T(8,128)S(1)} %get-tuple-element.48), channel_id=1, source_target_pairs={{0,16},{16,32},{32,48},{48,64},{64,80},{80,96},{96,112},{1,17},{17... | collective-permute-start | bytes 245768 | tf_op jit(solution)/shard_map/ppermute | solution.py:18
  19.1 4.7 %collective-permute-start.3 = (f32[5,10,1,128]{3,0,2,1:T(8,128)S(1)}, f32[5,10,1,128]{3,0,2,1:T(8,128)S(1)}, u32[]{:S(2)}, u32[]{:S(2)}) collective-permute-start(f32[5,10,1,128]{3,0,2,1:T(8,128)S(1)} %get-tuple-element.41), channel_id=1, source_target_pairs={{1,0},{2,1},{3,2},{4,3},{5,4},{6,5},{7,6},{8,7},{9,8},{10,9},{11,1... | collective-permute-start | bytes 76808 | tf_op jit(solution)/shard_map/ppermute | solution.py:21
  45.4 4.2 %collective-permute-start.4 = (f32[5,1,32,128]{3,0,2,1:T(8,128)S(1)}, f32[5,1,32,128]{3,0,2,1:T(8,128)S(1)}, u32[]{:S(2)}, u32[]{:S(2)}) collective-permute-start(f32[5,1,32,128]{3,0,2,1:T(8,128)S(1)} %get-tuple-element.46), channel_id=1, source_target_pairs={{0,16},{16,32},{32,48},{48,64},{64,80},{80,96},{96,112},{1,17},{17... | collective-permute-start | bytes 245768 | tf_op jit(solution)/shard_map/ppermute | solution.py:18
  52.1 3.8 %collective-permute-done.5 = f32[5,1,32,128]{3,0,2,1:T(8,128)S(1)} collective-permute-done((f32[5,1,32,128]{3,0,2,1:T(8,128)S(1)}, f32[5,1,32,128]{3,0,2,1:T(8,128)S(1)}, u32[]{:S(2)}, u32[]{:S(2)}) %collective-permute-start.5) | collective-permute-done | bytes 81952 | tf_op jit(solution)/shard_map/ppermute | solution.py:21
  58.7 5.4 %collective-permute-start.7 = (f32[5,10,1,128]{3,0,2,1:T(8,128)S(1)}, f32[5,10,1,128]{3,0,2,1:T(8,128)S(1)}, u32[]{:S(2)}, u32[]{:S(2)}) collective-permute-start(f32[5,10,1,128]{3,0,2,1:T(8,128)S(1)} %get-tuple-element.39), channel_id=1, source_target_pairs={{1,0},{2,1},{3,2},{4,3},{5,4},{6,5},{7,6},{8,7},{9,8},{10,9},{11,1... | collective-permute-start | bytes 76808 | tf_op jit(solution)/shard_map/ppermute | solution.py:21
  81.7 3.3 %broadcast_multiply_fusion = (f32[5,8,32,128]{3,0,2,1:T(8,128)S(1)}, f32[5,8,32,128]{3,0,2,1:T(8,128)}) fusion(f32[8,32,128]{2,1,0:T(8,128)S(1)} %convert_element_type.16, f32[5,8,32,128]{3,0,2,1:T(8,128)S(1)} %get-tuple-element.113, f32[5]{0:T(128)S(1)} %gather_fusion, f32[5,8,32,128]{3,0,2,1:T(8,128)S(1)} %convolution_bitcast_fusion.16, ...), kind=kOutput, calls=%fused_computation.510 | convolution fusion | flops 8519680 | bytes 18485760 | tf_op jit(solution)/shard_map/ab,bxyz->axyz/dot_general | solution.py:55
  89.9 3.7 %collective-permute-done.9 = f32[5,1,32,128]{3,0,2,1:T(8,128)S(1)} collective-permute-done((f32[5,1,32,128]{3,0,2,1:T(8,128)S(1)}, f32[5,1,32,128]{3,0,2,1:T(8,128)S(1)}, u32[]{:S(2)}, u32[]{:S(2)}) %collective-permute-start.9) | collective-permute-done | bytes 81952 | tf_op jit(solution)/shard_map/ppermute | solution.py:21
  93.7 3.4 %collective-permute-start.10 = (f32[5,10,1,128]{3,0,2,1:T(8,128)S(1)}, f32[5,10,1,128]{3,0,2,1:T(8,128)S(1)}, u32[]{:S(2)}, u32[]{:S(2)}) collective-permute-start(f32[5,10,1,128]{3,0,2,1:T(8,128)S(1)} %get-tuple-element.36), channel_id=1, source_target_pairs={{0,1},{1,2},{2,3},{3,4},{4,5},{5,6},{6,7},{7,8},{8,9},{9,10},{10,1... | collective-permute-start | bytes 76808 | tf_op jit(solution)/shard_map/ppermute | solution.py:18
  97.1 4.7 %collective-permute-start.11 = (f32[5,10,1,128]{3,0,2,1:T(8,128)S(1)}, f32[5,10,1,128]{3,0,2,1:T(8,128)S(1)}, u32[]{:S(2)}, u32[]{:S(2)}) collective-permute-start(f32[5,10,1,128]{3,0,2,1:T(8,128)S(1)} %get-tuple-element.37), channel_id=1, source_target_pairs={{1,0},{2,1},{3,2},{4,3},{5,4},{6,5},{7,6},{8,7},{9,8},{10,9},{11,1... | collective-permute-start | bytes 76808 | tf_op jit(solution)/shard_map/ppermute | solution.py:21
  126.7 4.3 %collective-permute-done.13 = f32[5,1,32,128]{3,0,2,1:T(8,128)S(1)} collective-permute-done((f32[5,1,32,128]{3,0,2,1:T(8,128)S(1)}, f32[5,1,32,128]{3,0,2,1:T(8,128)S(1)}, u32[]{:S(2)}, u32[]{:S(2)}) %collective-permute-start.13) | collective-permute-done | bytes 81952 | tf_op jit(solution)/shard_map/ppermute | solution.py:21
  131.0 3.5 %collective-permute-start.14 = (f32[5,10,1,128]{3,0,2,1:T(8,128)S(1)}, f32[5,10,1,128]{3,0,2,1:T(8,128)S(1)}, u32[]{:S(2)}, u32[]{:S(2)}) collective-permute-start(f32[5,10,1,128]{3,0,2,1:T(8,128)S(1)} %get-tuple-element.34), channel_id=1, source_target_pairs={{0,1},{1,2},{2,3},{3,4},{4,5},{5,6},{6,7},{7,8},{8,9},{9,10},{10,1... | collective-permute-start | bytes 76808 | tf_op jit(solution)/shard_map/ppermute | solution.py:18
  134.5 4.5 %collective-permute-start.15 = (f32[5,10,1,128]{3,0,2,1:T(8,128)S(1)}, f32[5,10,1,128]{3,0,2,1:T(8,128)S(1)}, u32[]{:S(2)}, u32[]{:S(2)}) collective-permute-start(f32[5,10,1,128]{3,0,2,1:T(8,128)S(1)} %get-tuple-element.35), channel_id=1, source_target_pairs={{1,0},{2,1},{3,2},{4,3},{5,4},{6,5},{7,6},{8,7},{9,8},{10,9},{11,1... | collective-permute-start | bytes 76808 | tf_op jit(solution)/shard_map/ppermute | solution.py:21
  145.2 3.6 %collective-permute-done.17 = f32[5,1,16,128]{3,0,2,1:T(8,128)S(1)} collective-permute-done((f32[5,1,16,128]{3,0,2,1:T(8,128)S(1)}, f32[5,1,16,128]{3,0,2,1:T(8,128)S(1)}, u32[]{:S(2)}, u32[]{:S(2)}) %collective-permute-start.17) | collective-permute-done | bytes 40992 | tf_op jit(solution)/shard_map/ppermute | solution.py:21
  148.8 3.5 %collective-permute-start.18 = (f32[5,6,1,128]{3,0,2,1:T(8,128)S(1)}, f32[5,6,1,128]{3,0,2,1:T(8,128)S(1)}, u32[]{:S(2)}, u32[]{:S(2)}) collective-permute-start(f32[5,6,1,128]{3,0,2,1:T(8,128)S(1)} %get-tuple-element.54), channel_id=1, source_target_pairs={{0,1},{1,2},{2,3},{3,4},{4,5},{5,6},{6,7},{7,8},{8,9},{9,10},{10,1... | collective-permute-start | bytes 46088 | tf_op jit(solution)/shard_map/ppermute | solution.py:18
  152.3 4.5 %collective-permute-start.19 = (f32[5,6,1,128]{3,0,2,1:T(8,128)S(1)}, f32[5,6,1,128]{3,0,2,1:T(8,128)S(1)}, u32[]{:S(2)}, u32[]{:S(2)}) collective-permute-start(f32[5,6,1,128]{3,0,2,1:T(8,128)S(1)} %get-tuple-element.55), channel_id=1, source_target_pairs={{1,0},{2,1},{3,2},{4,3},{5,4},{6,5},{7,6},{8,7},{9,8},{10,9},{11,1... | collective-permute-start | bytes 46088 | tf_op jit(solution)/shard_map/ppermute | solution.py:21
  170.5 3.6 %collective-permute-done.21 = f32[5,1,16,128]{3,0,2,1:T(8,128)S(1)} collective-permute-done((f32[5,1,16,128]{3,0,2,1:T(8,128)S(1)}, f32[5,1,16,128]{3,0,2,1:T(8,128)S(1)}, u32[]{:S(2)}, u32[]{:S(2)}) %collective-permute-start.21) | collective-permute-done | bytes 40992 | tf_op jit(solution)/shard_map/ppermute | solution.py:21
  174.1 3.4 %collective-permute-start.22 = (f32[5,6,1,128]{3,0,2,1:T(8,128)S(1)}, f32[5,6,1,128]{3,0,2,1:T(8,128)S(1)}, u32[]{:S(2)}, u32[]{:S(2)}) collective-permute-start(f32[5,6,1,128]{3,0,2,1:T(8,128)S(1)} %get-tuple-element.52), channel_id=1, source_target_pairs={{0,1},{1,2},{2,3},{3,4},{4,5},{5,6},{6,7},{7,8},{8,9},{9,10},{10,1... | collective-permute-start | bytes 46088 | tf_op jit(solution)/shard_map/ppermute | solution.py:18
  177.6 4.7 %collective-permute-start.23 = (f32[5,6,1,128]{3,0,2,1:T(8,128)S(1)}, f32[5,6,1,128]{3,0,2,1:T(8,128)S(1)}, u32[]{:S(2)}, u32[]{:S(2)}) collective-permute-start(f32[5,6,1,128]{3,0,2,1:T(8,128)S(1)} %get-tuple-element.53), channel_id=1, source_target_pairs={{1,0},{2,1},{3,2},{4,3},{5,4},{6,5},{7,6},{8,7},{9,8},{10,9},{11,1... | collective-permute-start | bytes 46088 | tf_op jit(solution)/shard_map/ppermute | solution.py:21
  195.7 3.6 %collective-permute-done.25 = f32[5,1,16,128]{3,0,2,1:T(8,128)S(1)} collective-permute-done((f32[5,1,16,128]{3,0,2,1:T(8,128)S(1)}, f32[5,1,16,128]{3,0,2,1:T(8,128)S(1)}, u32[]{:S(2)}, u32[]{:S(2)}) %collective-permute-start.25) | collective-permute-done | bytes 40992 | tf_op jit(solution)/shard_map/ppermute | solution.py:21
  199.3 3.4 %collective-permute-start.26 = (f32[5,6,1,128]{3,0,2,1:T(8,128)S(1)}, f32[5,6,1,128]{3,0,2,1:T(8,128)S(1)}, u32[]{:S(2)}, u32[]{:S(2)}) collective-permute-start(f32[5,6,1,128]{3,0,2,1:T(8,128)S(1)} %get-tuple-element.50), channel_id=1, source_target_pairs={{0,1},{1,2},{2,3},{3,4},{4,5},{5,6},{6,7},{7,8},{8,9},{9,10},{10,1... | collective-permute-start | bytes 46088 | tf_op jit(solution)/shard_map/ppermute | solution.py:18
  202.8 4.5 %collective-permute-start.27 = (f32[5,6,1,128]{3,0,2,1:T(8,128)S(1)}, f32[5,6,1,128]{3,0,2,1:T(8,128)S(1)}, u32[]{:S(2)}, u32[]{:S(2)}) collective-permute-start(f32[5,6,1,128]{3,0,2,1:T(8,128)S(1)} %get-tuple-element.51), channel_id=1, source_target_pairs={{1,0},{2,1},{3,2},{4,3},{5,4},{6,5},{7,6},{8,7},{9,8},{10,9},{11,1... | collective-permute-start | bytes 46088 | tf_op jit(solution)/shard_map/ppermute | solution.py:21
  216.4 3.4 %collective-permute-start.30 = (f32[5,4,1,128]{3,0,2,1:T(8,128)S(1)}, f32[5,4,1,128]{3,0,2,1:T(8,128)S(1)}, u32[]{:S(2)}, u32[]{:S(2)}) collective-permute-start(f32[5,4,1,128]{3,0,2,1:T(8,128)S(1)} %get-tuple-element.66), channel_id=1, source_target_pairs={{0,1},{1,2},{2,3},{3,4},{4,5},{5,6},{6,7},{7,8},{8,9},{9,10},{10,1... | collective-permute-start | bytes 30728 | tf_op jit(solution)/shard_map/ppermute | solution.py:18
  219.8 4.5 %collective-permute-start.31 = (f32[5,4,1,128]{3,0,2,1:T(8,128)S(1)}, f32[5,4,1,128]{3,0,2,1:T(8,128)S(1)}, u32[]{:S(2)}, u32[]{:S(2)}) collective-permute-start(f32[5,4,1,128]{3,0,2,1:T(8,128)S(1)} %get-tuple-element.67), channel_id=1, source_target_pairs={{1,0},{2,1},{3,2},{4,3},{5,4},{6,5},{7,6},{8,7},{9,8},{10,9},{11,1... | collective-permute-start | bytes 30728 | tf_op jit(solution)/shard_map/ppermute | solution.py:21
  235.0 3.3 %collective-permute-done.33 = f32[5,1,8,128]{3,0,2,1:T(8,128)S(1)} collective-permute-done((f32[5,1,8,128]{3,0,2,1:T(8,128)S(1)}, f32[5,1,8,128]{3,0,2,1:T(8,128)S(1)}, u32[]{:S(2)}, u32[]{:S(2)}) %collective-permute-start.33) | collective-permute-done | bytes 20512 | tf_op jit(solution)/shard_map/ppermute | solution.py:21
  238.3 3.4 %collective-permute-start.34 = (f32[5,4,1,128]{3,0,2,1:T(8,128)S(1)}, f32[5,4,1,128]{3,0,2,1:T(8,128)S(1)}, u32[]{:S(2)}, u32[]{:S(2)}) collective-permute-start(f32[5,4,1,128]{3,0,2,1:T(8,128)S(1)} %get-tuple-element.64), channel_id=1, source_target_pairs={{0,1},{1,2},{2,3},{3,4},{4,5},{5,6},{6,7},{7,8},{8,9},{9,10},{10,1... | collective-permute-start | bytes 30728 | tf_op jit(solution)/shard_map/ppermute | solution.py:18
  241.7 4.5 %collective-permute-start.35 = (f32[5,4,1,128]{3,0,2,1:T(8,128)S(1)}, f32[5,4,1,128]{3,0,2,1:T(8,128)S(1)}, u32[]{:S(2)}, u32[]{:S(2)}) collective-permute-start(f32[5,4,1,128]{3,0,2,1:T(8,128)S(1)} %get-tuple-element.65), channel_id=1, source_target_pairs={{1,0},{2,1},{3,2},{4,3},{5,4},{6,5},{7,6},{8,7},{9,8},{10,9},{11,1... | collective-permute-start | bytes 30728 | tf_op jit(solution)/shard_map/ppermute | solution.py:21
  260.2 3.4 %collective-permute-start.38 = (f32[5,4,1,128]{3,0,2,1:T(8,128)S(1)}, f32[5,4,1,128]{3,0,2,1:T(8,128)S(1)}, u32[]{:S(2)}, u32[]{:S(2)}) collective-permute-start(f32[5,4,1,128]{3,0,2,1:T(8,128)S(1)} %get-tuple-element.62), channel_id=1, source_target_pairs={{0,1},{1,2},{2,3},{3,4},{4,5},{5,6},{6,7},{7,8},{8,9},{9,10},{10,1... | collective-permute-start | bytes 30728 | tf_op jit(solution)/shard_map/ppermute | solution.py:18
  263.6 4.5 %collective-permute-start.39 = (f32[5,4,1,128]{3,0,2,1:T(8,128)S(1)}, f32[5,4,1,128]{3,0,2,1:T(8,128)S(1)}, u32[]{:S(2)}, u32[]{:S(2)}) collective-permute-start(f32[5,4,1,128]{3,0,2,1:T(8,128)S(1)} %get-tuple-element.63), channel_id=1, source_target_pairs={{1,0},{2,1},{3,2},{4,3},{5,4},{6,5},{7,6},{8,7},{9,8},{10,9},{11,1... | collective-permute-start | bytes 30728 | tf_op jit(solution)/shard_map/ppermute | solution.py:21
  276.9 3.4 %collective-permute-start.42 = (f32[5,3,1,128]{3,0,2,1:T(8,128)S(1)}, f32[5,3,1,128]{3,0,2,1:T(8,128)S(1)}, u32[]{:S(2)}, u32[]{:S(2)}) collective-permute-start(f32[5,3,1,128]{3,0,2,1:T(8,128)S(1)} %get-tuple-element.76), channel_id=1, source_target_pairs={{0,1},{1,2},{2,3},{3,4},{4,5},{5,6},{6,7},{7,8},{8,9},{9,10},{10,1... | collective-permute-start | bytes 23048 | tf_op jit(solution)/shard_map/ppermute | solution.py:18
  280.4 4.5 %collective-permute-start.43 = (f32[5,3,1,128]{3,0,2,1:T(8,128)S(1)}, f32[5,3,1,128]{3,0,2,1:T(8,128)S(1)}, u32[]{:S(2)}, u32[]{:S(2)}) collective-permute-start(f32[5,3,1,128]{3,0,2,1:T(8,128)S(1)} %get-tuple-element.77), channel_id=1, source_target_pairs={{1,0},{2,1},{3,2},{4,3},{5,4},{6,5},{7,6},{8,7},{9,8},{10,9},{11,1... | collective-permute-start | bytes 23048 | tf_op jit(solution)/shard_map/ppermute | solution.py:21
  297.9 3.4 %collective-permute-start.46 = (f32[5,3,1,128]{3,0,2,1:T(8,128)S(1)}, f32[5,3,1,128]{3,0,2,1:T(8,128)S(1)}, u32[]{:S(2)}, u32[]{:S(2)}) collective-permute-start(f32[5,3,1,128]{3,0,2,1:T(8,128)S(1)} %get-tuple-element.74), channel_id=1, source_target_pairs={{0,1},{1,2},{2,3},{3,4},{4,5},{5,6},{6,7},{7,8},{8,9},{9,10},{10,1... | collective-permute-start | bytes 23048 | tf_op jit(solution)/shard_map/ppermute | solution.py:18
  301.3 4.5 %collective-permute-start.47 = (f32[5,3,1,128]{3,0,2,1:T(8,128)S(1)}, f32[5,3,1,128]{3,0,2,1:T(8,128)S(1)}, u32[]{:S(2)}, u32[]{:S(2)}) collective-permute-start(f32[5,3,1,128]{3,0,2,1:T(8,128)S(1)} %get-tuple-element.75), channel_id=1, source_target_pairs={{1,0},{2,1},{3,2},{4,3},{5,4},{6,5},{7,6},{8,7},{9,8},{10,9},{11,1... | collective-permute-start | bytes 23048 | tf_op jit(solution)/shard_map/ppermute | solution.py:21
  (408 shorter events, 182.1 us)
Async XLA Ops:
  3.1 12.8 %collective-permute-start = (f32[5,1,32,128]{3,0,2,1:T(8,128)S(1)}, f32[5,1,32,128]{3,0,2,1:T(8,128)S(1)}, u32[]{:S(2)}, u32[]{:S(2)}) collective-permute-start(f32[5,1,32,128]{3,0,2,1:T(8,128)S(1)} %get-tuple-element.48), channel_id=1, source_target_pairs={{0,16},{16,32},{32,48},{48,64},{64,80},{80,96},{96,112},{1,17},{17... | collective-permute-start | bytes 245768 | tf_op jit(solution)/shard_map/ppermute | solution.py:18
  7.4 8.5 %collective-permute-start.1 = (f32[5,1,32,128]{3,0,2,1:T(8,128)S(1)}, f32[5,1,32,128]{3,0,2,1:T(8,128)S(1)}, u32[]{:S(2)}, u32[]{:S(2)}) collective-permute-start(f32[5,1,32,128]{3,0,2,1:T(8,128)S(1)} %get-tuple-element.49), channel_id=1, source_target_pairs={{16,0},{32,16},{48,32},{64,48},{80,64},{96,80},{112,96},{17,1},{33... | collective-permute-start | bytes 245768 | tf_op jit(solution)/shard_map/ppermute | solution.py:21
  15.9 9.0 %collective-permute-start.2 = (f32[5,10,1,128]{3,0,2,1:T(8,128)S(1)}, f32[5,10,1,128]{3,0,2,1:T(8,128)S(1)}, u32[]{:S(2)}, u32[]{:S(2)}) collective-permute-start(f32[5,10,1,128]{3,0,2,1:T(8,128)S(1)} %get-tuple-element.40), channel_id=1, source_target_pairs={{0,1},{1,2},{2,3},{3,4},{4,5},{5,6},{6,7},{7,8},{8,9},{9,10},{10,1... | collective-permute-start | bytes 76808 | tf_op jit(solution)/shard_map/ppermute | solution.py:18
  19.1 5.9 %collective-permute-start.3 = (f32[5,10,1,128]{3,0,2,1:T(8,128)S(1)}, f32[5,10,1,128]{3,0,2,1:T(8,128)S(1)}, u32[]{:S(2)}, u32[]{:S(2)}) collective-permute-start(f32[5,10,1,128]{3,0,2,1:T(8,128)S(1)} %get-tuple-element.41), channel_id=1, source_target_pairs={{1,0},{2,1},{3,2},{4,3},{5,4},{6,5},{7,6},{8,7},{9,8},{10,9},{11,1... | collective-permute-start | bytes 76808 | tf_op jit(solution)/shard_map/ppermute | solution.py:21
  45.4 6.7 %collective-permute-start.4 = (f32[5,1,32,128]{3,0,2,1:T(8,128)S(1)}, f32[5,1,32,128]{3,0,2,1:T(8,128)S(1)}, u32[]{:S(2)}, u32[]{:S(2)}) collective-permute-start(f32[5,1,32,128]{3,0,2,1:T(8,128)S(1)} %get-tuple-element.46), channel_id=1, source_target_pairs={{0,16},{16,32},{32,48},{48,64},{64,80},{80,96},{96,112},{1,17},{17... | collective-permute-start | bytes 245768 | tf_op jit(solution)/shard_map/ppermute | solution.py:18
  49.6 6.3 %collective-permute-start.5 = (f32[5,1,32,128]{3,0,2,1:T(8,128)S(1)}, f32[5,1,32,128]{3,0,2,1:T(8,128)S(1)}, u32[]{:S(2)}, u32[]{:S(2)}) collective-permute-start(f32[5,1,32,128]{3,0,2,1:T(8,128)S(1)} %get-tuple-element.47), channel_id=1, source_target_pairs={{16,0},{32,16},{48,32},{64,48},{80,64},{96,80},{112,96},{17,1},{33... | collective-permute-start | bytes 245768 | tf_op jit(solution)/shard_map/ppermute | solution.py:21
  55.9 9.3 %collective-permute-start.6 = (f32[5,10,1,128]{3,0,2,1:T(8,128)S(1)}, f32[5,10,1,128]{3,0,2,1:T(8,128)S(1)}, u32[]{:S(2)}, u32[]{:S(2)}) collective-permute-start(f32[5,10,1,128]{3,0,2,1:T(8,128)S(1)} %get-tuple-element.38), channel_id=1, source_target_pairs={{0,1},{1,2},{2,3},{3,4},{4,5},{5,6},{6,7},{7,8},{8,9},{9,10},{10,1... | collective-permute-start | bytes 76808 | tf_op jit(solution)/shard_map/ppermute | solution.py:18
  58.7 6.6 %collective-permute-start.7 = (f32[5,10,1,128]{3,0,2,1:T(8,128)S(1)}, f32[5,10,1,128]{3,0,2,1:T(8,128)S(1)}, u32[]{:S(2)}, u32[]{:S(2)}) collective-permute-start(f32[5,10,1,128]{3,0,2,1:T(8,128)S(1)} %get-tuple-element.39), channel_id=1, source_target_pairs={{1,0},{2,1},{3,2},{4,3},{5,4},{6,5},{7,6},{8,7},{9,8},{10,9},{11,1... | collective-permute-start | bytes 76808 | tf_op jit(solution)/shard_map/ppermute | solution.py:21
  87.4 6.3 %collective-permute-start.9 = (f32[5,1,32,128]{3,0,2,1:T(8,128)S(1)}, f32[5,1,32,128]{3,0,2,1:T(8,128)S(1)}, u32[]{:S(2)}, u32[]{:S(2)}) collective-permute-start(f32[5,1,32,128]{3,0,2,1:T(8,128)S(1)} %get-tuple-element.45), channel_id=1, source_target_pairs={{16,0},{32,16},{48,32},{64,48},{80,64},{96,80},{112,96},{17,1},{33... | collective-permute-start | bytes 245768 | tf_op jit(solution)/shard_map/ppermute | solution.py:21
  93.7 9.3 %collective-permute-start.10 = (f32[5,10,1,128]{3,0,2,1:T(8,128)S(1)}, f32[5,10,1,128]{3,0,2,1:T(8,128)S(1)}, u32[]{:S(2)}, u32[]{:S(2)}) collective-permute-start(f32[5,10,1,128]{3,0,2,1:T(8,128)S(1)} %get-tuple-element.36), channel_id=1, source_target_pairs={{0,1},{1,2},{2,3},{3,4},{4,5},{5,6},{6,7},{7,8},{8,9},{9,10},{10,1... | collective-permute-start | bytes 76808 | tf_op jit(solution)/shard_map/ppermute | solution.py:18
  97.1 5.9 %collective-permute-start.11 = (f32[5,10,1,128]{3,0,2,1:T(8,128)S(1)}, f32[5,10,1,128]{3,0,2,1:T(8,128)S(1)}, u32[]{:S(2)}, u32[]{:S(2)}) collective-permute-start(f32[5,10,1,128]{3,0,2,1:T(8,128)S(1)} %get-tuple-element.37), channel_id=1, source_target_pairs={{1,0},{2,1},{3,2},{4,3},{5,4},{6,5},{7,6},{8,7},{9,8},{10,9},{11,1... | collective-permute-start | bytes 76808 | tf_op jit(solution)/shard_map/ppermute | solution.py:21
  124.7 6.3 %collective-permute-start.13 = (f32[5,1,32,128]{3,0,2,1:T(8,128)S(1)}, f32[5,1,32,128]{3,0,2,1:T(8,128)S(1)}, u32[]{:S(2)}, u32[]{:S(2)}) collective-permute-start(f32[5,1,32,128]{3,0,2,1:T(8,128)S(1)} %get-tuple-element.43), channel_id=1, source_target_pairs={{16,0},{32,16},{48,32},{64,48},{80,64},{96,80},{112,96},{17,1},{33... | collective-permute-start | bytes 245768 | tf_op jit(solution)/shard_map/ppermute | solution.py:21
  131.0 8.5 %collective-permute-start.14 = (f32[5,10,1,128]{3,0,2,1:T(8,128)S(1)}, f32[5,10,1,128]{3,0,2,1:T(8,128)S(1)}, u32[]{:S(2)}, u32[]{:S(2)}) collective-permute-start(f32[5,10,1,128]{3,0,2,1:T(8,128)S(1)} %get-tuple-element.34), channel_id=1, source_target_pairs={{0,1},{1,2},{2,3},{3,4},{4,5},{5,6},{6,7},{7,8},{8,9},{9,10},{10,1... | collective-permute-start | bytes 76808 | tf_op jit(solution)/shard_map/ppermute | solution.py:18
  134.5 5.6 %collective-permute-start.15 = (f32[5,10,1,128]{3,0,2,1:T(8,128)S(1)}, f32[5,10,1,128]{3,0,2,1:T(8,128)S(1)}, u32[]{:S(2)}, u32[]{:S(2)}) collective-permute-start(f32[5,10,1,128]{3,0,2,1:T(8,128)S(1)} %get-tuple-element.35), channel_id=1, source_target_pairs={{1,0},{2,1},{3,2},{4,3},{5,4},{6,5},{7,6},{8,7},{9,8},{10,9},{11,1... | collective-permute-start | bytes 76808 | tf_op jit(solution)/shard_map/ppermute | solution.py:21
  143.2 5.6 %collective-permute-start.17 = (f32[5,1,16,128]{3,0,2,1:T(8,128)S(1)}, f32[5,1,16,128]{3,0,2,1:T(8,128)S(1)}, u32[]{:S(2)}, u32[]{:S(2)}) collective-permute-start(f32[5,1,16,128]{3,0,2,1:T(8,128)S(1)} %get-tuple-element.61), channel_id=1, source_target_pairs={{16,0},{32,16},{48,32},{64,48},{80,64},{96,80},{112,96},{17,1},{33... | collective-permute-start | bytes 122888 | tf_op jit(solution)/shard_map/ppermute | solution.py:21
  148.8 8.3 %collective-permute-start.18 = (f32[5,6,1,128]{3,0,2,1:T(8,128)S(1)}, f32[5,6,1,128]{3,0,2,1:T(8,128)S(1)}, u32[]{:S(2)}, u32[]{:S(2)}) collective-permute-start(f32[5,6,1,128]{3,0,2,1:T(8,128)S(1)} %get-tuple-element.54), channel_id=1, source_target_pairs={{0,1},{1,2},{2,3},{3,4},{4,5},{5,6},{6,7},{7,8},{8,9},{9,10},{10,1... | collective-permute-start | bytes 46088 | tf_op jit(solution)/shard_map/ppermute | solution.py:18
  152.3 5.5 %collective-permute-start.19 = (f32[5,6,1,128]{3,0,2,1:T(8,128)S(1)}, f32[5,6,1,128]{3,0,2,1:T(8,128)S(1)}, u32[]{:S(2)}, u32[]{:S(2)}) collective-permute-start(f32[5,6,1,128]{3,0,2,1:T(8,128)S(1)} %get-tuple-element.55), channel_id=1, source_target_pairs={{1,0},{2,1},{3,2},{4,3},{5,4},{6,5},{7,6},{8,7},{9,8},{10,9},{11,1... | collective-permute-start | bytes 46088 | tf_op jit(solution)/shard_map/ppermute | solution.py:21
  168.6 5.6 %collective-permute-start.21 = (f32[5,1,16,128]{3,0,2,1:T(8,128)S(1)}, f32[5,1,16,128]{3,0,2,1:T(8,128)S(1)}, u32[]{:S(2)}, u32[]{:S(2)}) collective-permute-start(f32[5,1,16,128]{3,0,2,1:T(8,128)S(1)} %get-tuple-element.59), channel_id=1, source_target_pairs={{16,0},{32,16},{48,32},{64,48},{80,64},{96,80},{112,96},{17,1},{33... | collective-permute-start | bytes 122888 | tf_op jit(solution)/shard_map/ppermute | solution.py:21
  174.1 8.4 %collective-permute-start.22 = (f32[5,6,1,128]{3,0,2,1:T(8,128)S(1)}, f32[5,6,1,128]{3,0,2,1:T(8,128)S(1)}, u32[]{:S(2)}, u32[]{:S(2)}) collective-permute-start(f32[5,6,1,128]{3,0,2,1:T(8,128)S(1)} %get-tuple-element.52), channel_id=1, source_target_pairs={{0,1},{1,2},{2,3},{3,4},{4,5},{5,6},{6,7},{7,8},{8,9},{9,10},{10,1... | collective-permute-start | bytes 46088 | tf_op jit(solution)/shard_map/ppermute | solution.py:18
  177.6 5.5 %collective-permute-start.23 = (f32[5,6,1,128]{3,0,2,1:T(8,128)S(1)}, f32[5,6,1,128]{3,0,2,1:T(8,128)S(1)}, u32[]{:S(2)}, u32[]{:S(2)}) collective-permute-start(f32[5,6,1,128]{3,0,2,1:T(8,128)S(1)} %get-tuple-element.53), channel_id=1, source_target_pairs={{1,0},{2,1},{3,2},{4,3},{5,4},{6,5},{7,6},{8,7},{9,8},{10,9},{11,1... | collective-permute-start | bytes 46088 | tf_op jit(solution)/shard_map/ppermute | solution.py:21
  193.7 5.6 %collective-permute-start.25 = (f32[5,1,16,128]{3,0,2,1:T(8,128)S(1)}, f32[5,1,16,128]{3,0,2,1:T(8,128)S(1)}, u32[]{:S(2)}, u32[]{:S(2)}) collective-permute-start(f32[5,1,16,128]{3,0,2,1:T(8,128)S(1)} %get-tuple-element.57), channel_id=1, source_target_pairs={{16,0},{32,16},{48,32},{64,48},{80,64},{96,80},{112,96},{17,1},{33... | collective-permute-start | bytes 122888 | tf_op jit(solution)/shard_map/ppermute | solution.py:21
  199.3 8.1 %collective-permute-start.26 = (f32[5,6,1,128]{3,0,2,1:T(8,128)S(1)}, f32[5,6,1,128]{3,0,2,1:T(8,128)S(1)}, u32[]{:S(2)}, u32[]{:S(2)}) collective-permute-start(f32[5,6,1,128]{3,0,2,1:T(8,128)S(1)} %get-tuple-element.50), channel_id=1, source_target_pairs={{0,1},{1,2},{2,3},{3,4},{4,5},{5,6},{6,7},{7,8},{8,9},{9,10},{10,1... | collective-permute-start | bytes 46088 | tf_op jit(solution)/shard_map/ppermute | solution.py:18
  202.8 5.5 %collective-permute-start.27 = (f32[5,6,1,128]{3,0,2,1:T(8,128)S(1)}, f32[5,6,1,128]{3,0,2,1:T(8,128)S(1)}, u32[]{:S(2)}, u32[]{:S(2)}) collective-permute-start(f32[5,6,1,128]{3,0,2,1:T(8,128)S(1)} %get-tuple-element.51), channel_id=1, source_target_pairs={{1,0},{2,1},{3,2},{4,3},{5,4},{6,5},{7,6},{8,7},{9,8},{10,9},{11,1... | collective-permute-start | bytes 46088 | tf_op jit(solution)/shard_map/ppermute | solution.py:21
  216.4 8.1 %collective-permute-start.30 = (f32[5,4,1,128]{3,0,2,1:T(8,128)S(1)}, f32[5,4,1,128]{3,0,2,1:T(8,128)S(1)}, u32[]{:S(2)}, u32[]{:S(2)}) collective-permute-start(f32[5,4,1,128]{3,0,2,1:T(8,128)S(1)} %get-tuple-element.66), channel_id=1, source_target_pairs={{0,1},{1,2},{2,3},{3,4},{4,5},{5,6},{6,7},{7,8},{8,9},{9,10},{10,1... | collective-permute-start | bytes 30728 | tf_op jit(solution)/shard_map/ppermute | solution.py:18
  219.8 5.4 %collective-permute-start.31 = (f32[5,4,1,128]{3,0,2,1:T(8,128)S(1)}, f32[5,4,1,128]{3,0,2,1:T(8,128)S(1)}, u32[]{:S(2)}, u32[]{:S(2)}) collective-permute-start(f32[5,4,1,128]{3,0,2,1:T(8,128)S(1)} %get-tuple-element.67), channel_id=1, source_target_pairs={{1,0},{2,1},{3,2},{4,3},{5,4},{6,5},{7,6},{8,7},{9,8},{10,9},{11,1... | collective-permute-start | bytes 30728 | tf_op jit(solution)/shard_map/ppermute | solution.py:21
  238.3 8.1 %collective-permute-start.34 = (f32[5,4,1,128]{3,0,2,1:T(8,128)S(1)}, f32[5,4,1,128]{3,0,2,1:T(8,128)S(1)}, u32[]{:S(2)}, u32[]{:S(2)}) collective-permute-start(f32[5,4,1,128]{3,0,2,1:T(8,128)S(1)} %get-tuple-element.64), channel_id=1, source_target_pairs={{0,1},{1,2},{2,3},{3,4},{4,5},{5,6},{6,7},{7,8},{8,9},{9,10},{10,1... | collective-permute-start | bytes 30728 | tf_op jit(solution)/shard_map/ppermute | solution.py:18
  241.7 5.4 %collective-permute-start.35 = (f32[5,4,1,128]{3,0,2,1:T(8,128)S(1)}, f32[5,4,1,128]{3,0,2,1:T(8,128)S(1)}, u32[]{:S(2)}, u32[]{:S(2)}) collective-permute-start(f32[5,4,1,128]{3,0,2,1:T(8,128)S(1)} %get-tuple-element.65), channel_id=1, source_target_pairs={{1,0},{2,1},{3,2},{4,3},{5,4},{6,5},{7,6},{8,7},{9,8},{10,9},{11,1... | collective-permute-start | bytes 30728 | tf_op jit(solution)/shard_map/ppermute | solution.py:21
  260.2 8.0 %collective-permute-start.38 = (f32[5,4,1,128]{3,0,2,1:T(8,128)S(1)}, f32[5,4,1,128]{3,0,2,1:T(8,128)S(1)}, u32[]{:S(2)}, u32[]{:S(2)}) collective-permute-start(f32[5,4,1,128]{3,0,2,1:T(8,128)S(1)} %get-tuple-element.62), channel_id=1, source_target_pairs={{0,1},{1,2},{2,3},{3,4},{4,5},{5,6},{6,7},{7,8},{8,9},{9,10},{10,1... | collective-permute-start | bytes 30728 | tf_op jit(solution)/shard_map/ppermute | solution.py:18
  263.6 5.4 %collective-permute-start.39 = (f32[5,4,1,128]{3,0,2,1:T(8,128)S(1)}, f32[5,4,1,128]{3,0,2,1:T(8,128)S(1)}, u32[]{:S(2)}, u32[]{:S(2)}) collective-permute-start(f32[5,4,1,128]{3,0,2,1:T(8,128)S(1)} %get-tuple-element.63), channel_id=1, source_target_pairs={{1,0},{2,1},{3,2},{4,3},{5,4},{6,5},{7,6},{8,7},{9,8},{10,9},{11,1... | collective-permute-start | bytes 30728 | tf_op jit(solution)/shard_map/ppermute | solution.py:21
  276.9 8.0 %collective-permute-start.42 = (f32[5,3,1,128]{3,0,2,1:T(8,128)S(1)}, f32[5,3,1,128]{3,0,2,1:T(8,128)S(1)}, u32[]{:S(2)}, u32[]{:S(2)}) collective-permute-start(f32[5,3,1,128]{3,0,2,1:T(8,128)S(1)} %get-tuple-element.76), channel_id=1, source_target_pairs={{0,1},{1,2},{2,3},{3,4},{4,5},{5,6},{6,7},{7,8},{8,9},{9,10},{10,1... | collective-permute-start | bytes 23048 | tf_op jit(solution)/shard_map/ppermute | solution.py:18
  297.9 10.2 %collective-permute-start.46 = (f32[5,3,1,128]{3,0,2,1:T(8,128)S(1)}, f32[5,3,1,128]{3,0,2,1:T(8,128)S(1)}, u32[]{:S(2)}, u32[]{:S(2)}) collective-permute-start(f32[5,3,1,128]{3,0,2,1:T(8,128)S(1)} %get-tuple-element.74), channel_id=1, source_target_pairs={{0,1},{1,2},{2,3},{3,4},{4,5},{5,6},{6,7},{7,8},{8,9},{9,10},{10,1... | collective-permute-start | bytes 23048 | tf_op jit(solution)/shard_map/ppermute | solution.py:18
  301.3 6.8 %collective-permute-start.47 = (f32[5,3,1,128]{3,0,2,1:T(8,128)S(1)}, f32[5,3,1,128]{3,0,2,1:T(8,128)S(1)}, u32[]{:S(2)}, u32[]{:S(2)}) collective-permute-start(f32[5,3,1,128]{3,0,2,1:T(8,128)S(1)} %get-tuple-element.75), channel_id=1, source_target_pairs={{1,0},{2,1},{3,2},{4,3},{5,4},{6,5},{7,6},{8,7},{9,8},{10,9},{11,1... | collective-permute-start | bytes 23048 | tf_op jit(solution)/shard_map/ppermute | solution.py:21
  (22 other events, 136.0 us)
